TPU v7x, 128 devices: a whole 4x4x4 slice. The times are simulated.
128 devices in a mesh: lon: 16 (over y, z_hi, core), lat: 8 (over x, z_lo).
Axes of the slice: x: 4, y: 4, z: 4 (z_hi: 2, z_lo: 2; z = z_hi * 2 + z_lo), core: 2. Of those that a mesh axis runs over, the one named last changes fastest.
Arguments:
- innovations: float32 [150, 65536], P(None, ('lon', 'lat')), may hold values from -6 to 6
- owner_tile: int32 [65536, 1], P(('lon', 'lat')), may hold values from 0 to 127; in each aligned block of 512 rows (0 to 511, 512 to 1023, ...) at most 16 rows name the same one
- obs_column: int32 [65536], P(('lon', 'lat')), may hold values from 0 to 8191
- obs_depth: int32 [65536], P(('lon', 'lat')), may hold values from 1 to 75
- coefficients: float32 [9, 512, 2048], P(None, 'lat', 'lon'), may hold values from 0.03 to 0.25
- sea_depth: int32 [512, 2048], P('lat', 'lon'), may hold values from 0 to 75
- balance: float32 [150, 150], replicated, may hold values from -0.5 to 0.5
Outputs:
- gradient: float32 [150, 512, 2048], P(None, 'lat', 'lon')
Inputs may be any that keep to these rules, and one draw needn't show every extreme that they name: `owner_tile`: among the 512 profiles of one device, at most 16 share one owner tile, and some device holds exactly 16 for one owner.
All inputs are finite; a program needn't handle non-finite values.
Results may differ from a plain program's by a relative error of at most 0.00012.
Values sent between devices are 32-bit elements; how exact they have to be, the bound alone decides.
No kernel may reach another device: no remote copies, remote signals or barrier semaphores. Data moves between devices by JAX's collectives and lax.ppermute only.
A program may use at most 128 MiB of HBM per device.

v0:
```python
import jax
import jax.numpy as jnp
from jax import lax
from jax.experimental import pallas as pl
from jax.experimental.pallas import tpu as pltpu
from jax.sharding import PartitionSpec as P

LEVELS = 75
PASSES = 4
RADIUS = PASSES
LANES = 256
CPAD = 152
CHUNK = 8
SPAD = 16


def shift_lon(block, step):
    count = lax.axis_size("lon")
    return lax.ppermute(block, "lon", [(i, (i + step) % count) for i in range(count)])


def shift_lat(block, step):
    count = lax.axis_size("lat")
    return lax.ppermute(
        block, "lat", [(i, i + step) for i in range(count) if 0 <= i + step < count]
    )


def shift_both(block, step_lon, step_lat):
    n_lon = lax.axis_size("lon")
    n_lat = lax.axis_size("lat")
    pairs = []
    for i in range(n_lon):
        for j in range(n_lat):
            if 0 <= j + step_lat < n_lat:
                pairs.append((i * n_lat + j, ((i + step_lon) % n_lon) * n_lat + j + step_lat))
    return lax.ppermute(block, ("lon", "lat"), pairs)


DIRECTIONS = (
    ("west", lambda v, r: v[:, :, v.shape[2] - r :], "lon", 1, 0),
    ("east", lambda v, r: v[:, :, :r], "lon", -1, 0),
    ("south", lambda v, r: v[v.shape[0] - r :], "lat", 0, 1),
    ("north", lambda v, r: v[:r], "lat", 0, -1),
    ("sw", lambda v, r: v[v.shape[0] - r :, :, v.shape[2] - r :], "both", 1, 1),
    ("se", lambda v, r: v[v.shape[0] - r :, :, :r], "both", -1, 1),
    ("nw", lambda v, r: v[:r, :, v.shape[2] - r :], "both", 1, -1),
    ("ne", lambda v, r: v[:r, :, :r], "both", -1, -1),
)


def exchange(parts):
    got = [dict() for _ in parts]
    for name, take, axis, step_lon, step_lat in DIRECTIONS:
        pieces = [take(v, RADIUS) for v in parts]
        flat = jnp.concatenate([p.reshape(-1) for p in pieces])
        if axis == "lon":
            flat = shift_lon(flat, step_lon)
        elif axis == "lat":
            flat = shift_lat(flat, step_lat)
        else:
            flat = shift_both(flat, step_lon, step_lat)
        offset = 0
        for i, p in enumerate(pieces):
            got[i][name] = flat[offset : offset + p.size].reshape(p.shape)
            offset += p.size
    return got


def field_halos(f):
    rows, cols, _ = f.shape
    r = RADIUS
    v_top = jnp.transpose(f[:r], (0, 2, 1))
    v_bot = jnp.transpose(f[rows - r :], (0, 2, 1))

    def t(a):
        return jnp.transpose(a, (0, 2, 1))

    return {
        "west": shift_lon(f[:, cols - r :, :], 1),
        "east": shift_lon(f[:, :r, :], -1),
        "south": shift_lat(v_bot, 1),
        "north": shift_lat(v_top, -1),
        "sw": t(shift_both(f[rows - r :, cols - r :, :], 1, 1)),
        "se": t(shift_both(f[rows - r :, :r, :], -1, 1)),
        "nw": t(shift_both(f[:r, cols - r :, :], 1, -1)),
        "ne": t(shift_both(f[:r, :r, :], -1, -1)),
    }


def side_lanes(east, west, gap):
    zeros = jnp.zeros(east.shape[:2] + (gap,), jnp.float32)
    return jnp.concatenate([east, zeros, west], axis=2)


def assemble(v, h):
    cols = v.shape[2]
    gap = LANES - cols - 2 * RADIUS
    top = jnp.concatenate([h["south"], side_lanes(h["se"], h["sw"], gap)], axis=2)
    mid = jnp.concatenate([v, side_lanes(h["east"], h["west"], gap)], axis=2)
    bot = jnp.concatenate([h["north"], side_lanes(h["ne"], h["nw"], gap)], axis=2)
    return jnp.concatenate([top, mid, bot], axis=0)


def split_bf16(x):
    hi = x.astype(jnp.bfloat16)
    lo = (x - hi.astype(jnp.float32)).astype(jnp.bfloat16)
    return hi, lo


def passes_kernel(
    v_ref, ew_ref, top_ref, bot_ref, lvl_ref, bal_ref, out_ref, a_ref, b_ref, p_ref, s_ref, u_ref
):
    full = p_ref.shape[0]
    rows = v_ref.shape[0]
    cols = v_ref.shape[1]
    chans = p_ref.shape[1]
    out_ch = out_ref.shape[1]
    statc = s_ref.shape[1]
    p_ref[:RADIUS] = top_ref[:, :chans, :]
    s_ref[:RADIUS] = top_ref[:, chans:, :]
    p_ref[full - RADIUS :] = bot_ref[:, :chans, :]
    s_ref[full - RADIUS :] = bot_ref[:, chans:, :]

    def fill(y, carry):
        body = jnp.transpose(v_ref[y])
        sides = jnp.transpose(ew_ref[y])
        for ref, lo, n in ((p_ref, 0, chans), (s_ref, chans, statc)):
            ref[y + RADIUS, :, :cols] = body[lo : lo + n]
            ref[y + RADIUS, :, cols:] = jnp.zeros((n, LANES - cols), jnp.float32)
            ref[y + RADIUS, :, cols : cols + RADIUS] = sides[lo : lo + n, :RADIUS]
            ref[y + RADIUS, :, LANES - RADIUS :] = sides[lo : lo + n, RADIUS:]
        return carry

    lax.fori_loop(0, rows, fill, 0)
    b_hi, b_lo = split_bf16(bal_ref[...])
    srcs = [p_ref, a_ref, b_ref, a_ref]
    dsts = [a_ref, b_ref, a_ref, None]
    for p in range(PASSES):
        src = srcs[p]
        dst = dsts[p]

        def row(y, carry, src=src, dst=dst):
            srows = [s_ref[y - dy] for dy in (-1, 0, 1)]
            coefs = {}
            for dy in (-1, 0, 1):
                for dx in (-1, 0, 1):
                    k = (dy + 1) * 3 + dx + 1
                    coefs[(dy, dx)] = jnp.broadcast_to(
                        srows[dy + 1][k : k + 1, :], (CHUNK, LANES)
                    )
            depth = jnp.broadcast_to(srows[1][9:10, :], (CHUNK, LANES))
            for c0 in range(0, chans, CHUNK):
                sums = [None, None, None]
                for dy in (-1, 0, 1):
                    v = src[y - dy, c0 : c0 + CHUNK, :]
                    for dx in (-1, 0, 1):
                        t = coefs[(dy, dx)] * v
                        sums[dx + 1] = t if sums[dx + 1] is None else sums[dx + 1] + t
                acc = (
                    sums[1]
                    + pltpu.roll(sums[0], LANES - 1, 1)
                    + pltpu.roll(sums[2], 1, 1)
                )
                u_ref[c0 : c0 + CHUNK, :] = jnp.where(
                    lvl_ref[c0 : c0 + CHUNK, :] < depth, acc, 0.0
                )
            u_hi, u_lo = split_bf16(u_ref[...])
            res = jnp.dot(b_hi, u_hi, preferred_element_type=jnp.float32)
            res = res + jnp.dot(b_hi, u_lo, preferred_element_type=jnp.float32)
            res = res + jnp.dot(b_lo, u_hi, preferred_element_type=jnp.float32)
            if dst is None:
                out_ref[y - RADIUS] = res[:out_ch, :cols]
            else:
                dst[y] = res
            return carry

        lax.fori_loop(p + 1, full - 1 - p, row, 0, unroll=2)


def run_passes(field, halos, balance, chans):
    rows, cols, cpad = field.shape
    full = rows + 2 * RADIUS
    gap = LANES - cols - 2 * RADIUS
    ew = jnp.concatenate([halos["east"], halos["west"]], axis=1)
    top = jnp.concatenate([halos["south"], side_lanes(halos["se"], halos["sw"], gap)], axis=2)
    bot = jnp.concatenate([halos["north"], side_lanes(halos["ne"], halos["nw"], gap)], axis=2)
    lvl = jnp.broadcast_to(
        (jnp.arange(CPAD) % LEVELS).astype(jnp.float32)[:, None], (CPAD, LANES)
    )
    bal_t = jnp.pad(balance.T, ((0, CPAD - chans), (0, CPAD - chans)))
    vmem = pltpu.VMEM
    work = full * CPAD * LANES
    return pl.pallas_call(
        passes_kernel,
        out_shape=jax.ShapeDtypeStruct((rows, chans, cols), jnp.float32),
        in_specs=[pl.BlockSpec(memory_space=vmem)] * 6,
        out_specs=pl.BlockSpec(memory_space=vmem),
        scratch_shapes=[
            vmem((full, CPAD, LANES), jnp.float32),
            vmem((full, CPAD, LANES), jnp.float32),
            vmem((full, CPAD, LANES), jnp.float32),
            vmem((full, SPAD, LANES), jnp.float32),
            vmem((CPAD, LANES), jnp.float32),
        ],
        compiler_params=pltpu.CompilerParams(vmem_limit_bytes=62 * 1024 * 1024),
        cost_estimate=pl.CostEstimate(
            flops=PASSES * (work * 20 + 6 * full * CPAD * CPAD * LANES),
            bytes_accessed=4 * (work + rows * chans * cols),
            transcendentals=0,
        ),
    )(field, ew, top, bot, lvl, bal_t)


def local(innovations, owner_tile, obs_column, obs_depth, coefficients, sea_depth, balance):
    channels = innovations.shape[0]
    obs_count = innovations.shape[1]
    devices = lax.axis_size("lon") * lax.axis_size("lat")
    capacity = 4 * obs_count // devices
    rows_y = sea_depth.shape[0]
    cols_x = sea_depth.shape[1]

    stat = jnp.concatenate([coefficients, sea_depth.astype(jnp.float32)[None]], axis=0)
    stat = jnp.transpose(stat, (1, 2, 0)).reshape(rows_y * cols_x, stat.shape[0])
    base = jnp.concatenate(
        [
            jnp.zeros((rows_y * cols_x, CPAD), jnp.float32),
            stat,
            jnp.zeros((rows_y * cols_x, SPAD - stat.shape[1]), jnp.float32),
        ],
        axis=1,
    )

    level_ids = jnp.arange(channels) % LEVELS
    kept = jnp.where(level_ids[:, None] < obs_depth[None, :], innovations, 0.0)
    targets = owner_tile[:, 0]
    one_hot = (targets[:, None] == jnp.arange(devices, dtype=jnp.int32)[None, :]).astype(jnp.int32)
    before = jnp.cumsum(one_hot, axis=0) - one_hot
    slot_rank = jnp.sum(before * one_hot, axis=1)
    destination = targets * capacity + slot_rank
    payload = jnp.concatenate(
        [
            kept.T,
            jnp.zeros((obs_count, CPAD - channels - 1), jnp.float32),
            obs_column.astype(jnp.float32)[:, None],
        ],
        axis=1,
    )
    send = jnp.zeros((devices * capacity, CPAD), jnp.float32).at[destination].set(payload)
    got = lax.all_to_all(
        send.reshape(devices, capacity, CPAD), ("lon", "lat"), 0, 0, tiled=True
    ).reshape(devices * capacity, CPAD)
    where = got[:, CPAD - 1].astype(jnp.int32)
    got = jnp.pad(got, ((0, 0), (0, SPAD)))
    field = base.at[where].add(got)
    field = field.reshape(rows_y, cols_x, CPAD + SPAD)
    out = run_passes(field, field_halos(field), balance, channels)
    return jnp.transpose(out, (1, 0, 2))


def solution(mesh):
    placed = (
        P(None, ("lon", "lat")),
        P(("lon", "lat"), None),
        P(("lon", "lat")),
        P(("lon", "lat")),
        P(None, "lat", "lon"),
        P("lat", "lon"),
        P(),
    )
    return jax.shard_map(
        local, mesh=mesh, in_specs=placed, out_specs=P(None, "lat", "lon"), check_vma=False
    )
```

profile of v0, /device:TPU:34, one launch (start us, length us, event | category | flops | bytes accessed | tf_op | source)
XLA Modules:
  0.0 221.1 jit_solution(321289783496498512)
XLA Ops:
  0.0 0.8 copy.30
  0.8 0.2 fusion.7
  1.1 0.9 fusion.6
  2.0 0.7 compare_select_fusion.1
  2.7 0.7 convert_element_type.31
  3.4 0.1 pad.21.clone
  3.5 1.1 select_bitcast_fusion
  4.6 0.1 pad_maximum_fusion.3
  4.7 0.2 copy.32
  4.9 3.7 %scatter_custom_fusion = f32[2048,152]{1,0:T(8,128)} fusion(s32[512]{0:T(512)S(1)} %bitcast.63, f32[512,152]{1,0:T(8,128)S(1)} %copy.32, f32[]{:T(128)} %constant.13.clone.1), kind=kCustom, calls=%fused_computation.8 | custom fusion | bytes 1245188 | tf_op jit(solution)/shard_map/scatter | solution.py:249
  8.6 10.2 %all-to-all-start = ((f32[128,16,152]{2,1,0:T(8,128)}), f32[128,16,152]{2,1,0:T(8,128)S(1)}, u32[]{:S(2)}, u32[]{:S(2)}) async-start(f32[128,16,152]{2,1,0:T(8,128)} %bitcast.45), calls=%async_computation | async-start | bytes 4194304 | tf_op jit(solution)/shard_map/all_to_all | solution.py:250
  18.9 2.7 %copy.29 = f32[64,128,10]{2,1,0:T(8,128)} copy(f32[64,128,10]{1,0,2:T(8,128)S(1)} %maximum_bitcast_fusion) | data formatting | bytes 655360 | tf_op jit(solution)/shard_map/transpose | solution.py:224
  21.6 0.1 pad.25.clone
  21.7 6.8 %maximum_maximum_fusion = f32[8192,168]{1,0:T(8,128)} fusion(f32[8192,10]{1,0:T(8,128)} %bitcast.39, f32[168]{0:T(256)S(1)} %pad.25.clone, f32[168]{0:T(256)S(1)} %pad.23.clone), kind=kLoop, calls=%fused_computation.2 | loop fusion | flops 2752512 | bytes 5834048 | tf_op jit(solution)/shard_map/concatenate | solution.py:225
  28.5 19.0 %all-to-all-done = f32[128,16,152]{2,1,0:T(8,128)S(1)} async-done(((f32[128,16,152]{2,1,0:T(8,128)}), f32[128,16,152]{2,1,0:T(8,128)S(1)}, u32[]{:S(2)}, u32[]{:S(2)}) %all-to-all-start) | async-done | bytes 1245216 | tf_op jit(solution)/shard_map/all_to_all | solution.py:250
  47.5 0.6 fusion.2
  48.1 19.4 %scatter_custom_fusion.1 = f32[8192,168]{1,0:T(8,128)} fusion(f32[8192,168]{1,0:T(8,128)} %maximum_maximum_fusion, s32[2048]{0:T(1024)S(1)} %fusion.2, f32[2048,152]{1,0:T(8,128)S(1)} %bitcast.41, f32[]{:T(128)} %constant.13.clone.1), kind=kCustom, calls=%fused_computation.4 | custom fusion | flops 344064 | bytes 7602688 | tf_op jit(solution)/shard_map/scatter-add | solution.py:255
  67.6 1.3 fusion.11
  68.9 0.2 copy.37
  69.1 2.3 %collective-permute-start.2 = (f32[4,168,128]{2,1,0:T(8,128)S(1)}, f32[4,168,128]{2,1,0:T(8,128)S(1)}, u32[]{:S(2)}, u32[]{:S(2)}) collective-permute-start(f32[4,168,128]{2,1,0:T(8,128)S(1)} %bitcast.56), channel_id=1, source_target_pairs={{0,1},{1,2},{2,3},{3,4},{4,5},{5,6},{6,7},{8,9},{9,10},{10,11},{11... | collective-permute-start | bytes 1032200 | tf_op jit(solution)/shard_map/ppermute | solution.py:24
  71.4 0.2 copy.41
  71.6 3.6 %collective-permute-start.5 = (f32[4,168,128]{2,1,0:T(8,128)S(1)}, f32[4,168,128]{2,1,0:T(8,128)S(1)}, u32[]{:S(2)}, u32[]{:S(2)}) collective-permute-start(f32[4,168,128]{2,1,0:T(8,128)S(1)} %bitcast.57), channel_id=1, source_target_pairs={{1,0},{2,1},{3,2},{4,3},{5,4},{6,5},{7,6},{9,8},{10,9},{11,10},{12... | collective-permute-start | bytes 1032200 | tf_op jit(solution)/shard_map/ppermute | solution.py:24
  75.1 2.1 fusion.13
  77.2 0.0 collective-permute-start
  77.2 0.5 collective-permute-start.1
  77.7 0.8 fusion.12
  78.6 0.2 copy.53
  78.7 7.2 %collective-permute-start.3 = (f32[4,4,168]{1,2,0:T(8,128)S(1)}, f32[4,4,168]{1,2,0:T(8,128)S(1)}, u32[]{:S(2)}, u32[]{:S(2)}) collective-permute-start(f32[4,4,168]{1,2,0:T(8,128)S(1)} %copy.53), channel_id=1, source_target_pairs={{0,121},{1,122},{2,123},{3,124},{4,125},{5,126},{6,127},{8,1},{9,2... | collective-permute-start | bytes 32264 | tf_op jit(solution)/shard_map/ppermute | solution.py:37
  86.0 0.1 pad.16.clone
  86.1 0.1 copy.44
  86.2 0.7 pad.9.bal_ref
  86.8 0.2 copy.54
  87.0 0.2 copy.55
  87.2 0.2 copy.56
  87.4 7.9 %collective-permute-done.3 = f32[4,4,168]{1,2,0:T(8,128)S(1)} collective-permute-done((f32[4,4,168]{1,2,0:T(8,128)S(1)}, f32[4,4,168]{1,2,0:T(8,128)S(1)}, u32[]{:S(2)}, u32[]{:S(2)}) %collective-permute-start.3) | collective-permute-done | bytes 10784 | tf_op jit(solution)/shard_map/ppermute | solution.py:37
  95.3 6.3 %collective-permute-start.4 = (f32[4,4,168]{1,2,0:T(8,128)S(1)}, f32[4,4,168]{1,2,0:T(8,128)S(1)}, u32[]{:S(2)}, u32[]{:S(2)}) collective-permute-start(f32[4,4,168]{1,2,0:T(8,128)S(1)} %copy.54), channel_id=1, source_target_pairs={{0,9},{1,10},{2,11},{3,12},{4,13},{5,14},{6,15},{8,17},{9,18},{10,... | collective-permute-start | bytes 32264 | tf_op jit(solution)/shard_map/ppermute | solution.py:37
  101.6 0.0 collective-permute-done
  101.6 1.9 collective-permute-start.6
  103.6 0.0 collective-permute-done.1
  103.6 2.1 collective-permute-start.7
  105.7 1.9 pad_maximum_fusion.2.ew_ref
  107.6 6.4 %collective-permute-done.6 = f32[4,4,168]{1,2,0:T(8,128)S(1)} collective-permute-done((f32[4,4,168]{1,2,0:T(8,128)S(1)}, f32[4,4,168]{1,2,0:T(8,128)S(1)}, u32[]{:S(2)}, u32[]{:S(2)}) %collective-permute-start.6) | collective-permute-done | bytes 10784 | tf_op jit(solution)/shard_map/ppermute | solution.py:37
  114.0 6.8 %collective-permute-done.7 = f32[4,4,168]{1,2,0:T(8,128)S(1)} collective-permute-done((f32[4,4,168]{1,2,0:T(8,128)S(1)}, f32[4,4,168]{1,2,0:T(8,128)S(1)}, u32[]{:S(2)}, u32[]{:S(2)}) %collective-permute-start.7) | collective-permute-done | bytes 10784 | tf_op jit(solution)/shard_map/ppermute | solution.py:37
  120.8 0.0 collective-permute-done.2
  120.8 1.4 pad_maximum_fusion.1
  122.2 0.8 broadcast_in_dim.40.lvl_ref
  122.9 92.6 %shard_map.73 = f32[64,150,128]{2,1,0:T(8,128)} custom-call(f32[64,128,168]{2,1,0:T(8,128)} %bitcast.44, f32[64,8,168]{2,1,0:T(8,128)} %pad_maximum_fusion.2.ew_ref, f32[4,168,256]{2,1,0:T(8,128)} %get-tuple-element.14.top_ref, f32[4,168,256]{2,1,0:T(8,128)} %get-tuple-element.13.bot_ref, f32[152,256]{1,0:T(8,128)} %broadcast_in_dim.40.lvl_ref, ...), custom_call_target="tpu_custom_call" | custom-call | flops 10444603392 | bytes 16121856 | tf_op jit(solution)/shard_map/pallas_call | solution.py:194
  215.5 5.6 %copy.46 = f32[150,64,128]{2,1,0:T(8,128)} copy(f32[150,64,128]{2,0,1:T(8,128)} %bitcast.46) | data formatting | bytes 9830400 | tf_op jit(solution)/shard_map/transpose | solution.py:258
  (22 shorter events, 0.2 us)
Async XLA Ops:
  3.4 15.4 %copy-start.2 = (s32[64,128]{1,0:T(8,128)S(1)}, s32[64,128]{1,0:T(8,128)}, u32[]{:S(2)}) copy-start(s32[64,128]{1,0:T(8,128)} %param.12) | copy-start | bytes 98308
  3.5 15.4 %copy-start = (f32[9,64,128]{2,1,0:T(8,128)S(1)}, f32[9,64,128]{2,1,0:T(8,128)}, u32[]{:S(2)}) copy-start(f32[9,64,128]{2,1,0:T(8,128)} %param.11) | copy-start | bytes 884740
  8.6 38.9 %all-to-all-start = ((f32[128,16,152]{2,1,0:T(8,128)}), f32[128,16,152]{2,1,0:T(8,128)S(1)}, u32[]{:S(2)}, u32[]{:S(2)}) async-start(f32[128,16,152]{2,1,0:T(8,128)} %bitcast.45), calls=%async_computation | async-start | bytes 4194304 | tf_op jit(solution)/shard_map/all_to_all | solution.py:250
  67.6 18.5 %copy-start.1 = (f32[150,150]{1,0:T(8,128)S(1)}, f32[150,150]{1,0:T(8,128)}, u32[]{:S(2)}) copy-start(f32[150,150]{1,0:T(8,128)} %param.13) | copy-start | bytes 270004
  69.1 51.7 %collective-permute-start.2 = (f32[4,168,128]{2,1,0:T(8,128)S(1)}, f32[4,168,128]{2,1,0:T(8,128)S(1)}, u32[]{:S(2)}, u32[]{:S(2)}) collective-permute-start(f32[4,168,128]{2,1,0:T(8,128)S(1)} %bitcast.56), channel_id=1, source_target_pairs={{0,1},{1,2},{2,3},{3,4},{4,5},{5,6},{6,7},{8,9},{9,10},{10,11},{11... | collective-permute-start | bytes 1032200 | tf_op jit(solution)/shard_map/ppermute | solution.py:24
  71.6 49.2 %collective-permute-start.5 = (f32[4,168,128]{2,1,0:T(8,128)S(1)}, f32[4,168,128]{2,1,0:T(8,128)S(1)}, u32[]{:S(2)}, u32[]{:S(2)}) collective-permute-start(f32[4,168,128]{2,1,0:T(8,128)S(1)} %bitcast.57), channel_id=1, source_target_pairs={{1,0},{2,1},{3,2},{4,3},{5,4},{6,5},{7,6},{9,8},{10,9},{11,10},{12... | collective-permute-start | bytes 1032200 | tf_op jit(solution)/shard_map/ppermute | solution.py:24
  77.2 24.4 %collective-permute-start = (f32[64,4,168]{2,1,0:T(4,128)}, f32[64,4,168]{2,1,0:T(4,128)S(1)}, u32[]{:S(2)}, u32[]{:S(2)}) collective-permute-start(f32[64,4,168]{2,1,0:T(4,128)} %get-tuple-element.11), channel_id=1, source_target_pairs={{0,120},{8,0},{16,8},{24,16},{32,24},{40,32},{48,40},{56,48},{64,5... | collective-permute-start | bytes 516104 | tf_op jit(solution)/shard_map/ppermute | solution.py:19
  77.2 26.3 %collective-permute-start.1 = (f32[64,4,168]{2,1,0:T(4,128)}, f32[64,4,168]{2,1,0:T(4,128)}, u32[]{:S(2)}, u32[]{:S(2)}) collective-permute-start(f32[64,4,168]{2,1,0:T(4,128)} %get-tuple-element.12), channel_id=1, source_target_pairs={{0,8},{8,16},{16,24},{24,32},{32,40},{40,48},{48,56},{56,64},{64,7... | collective-permute-start | bytes 516104 | tf_op jit(solution)/shard_map/ppermute | solution.py:19
  78.7 16.6 %collective-permute-start.3 = (f32[4,4,168]{1,2,0:T(8,128)S(1)}, f32[4,4,168]{1,2,0:T(8,128)S(1)}, u32[]{:S(2)}, u32[]{:S(2)}) collective-permute-start(f32[4,4,168]{1,2,0:T(8,128)S(1)} %copy.53), channel_id=1, source_target_pairs={{0,121},{1,122},{2,123},{3,124},{4,125},{5,126},{6,127},{8,1},{9,2... | collective-permute-start | bytes 32264 | tf_op jit(solution)/shard_map/ppermute | solution.py:37
  95.3 12.2 %collective-permute-start.4 = (f32[4,4,168]{1,2,0:T(8,128)S(1)}, f32[4,4,168]{1,2,0:T(8,128)S(1)}, u32[]{:S(2)}, u32[]{:S(2)}) collective-permute-start(f32[4,4,168]{1,2,0:T(8,128)S(1)} %copy.54), channel_id=1, source_target_pairs={{0,9},{1,10},{2,11},{3,12},{4,13},{5,14},{6,15},{8,17},{9,18},{10,... | collective-permute-start | bytes 32264 | tf_op jit(solution)/shard_map/ppermute | solution.py:37
  101.6 12.3 %collective-permute-start.6 = (f32[4,4,168]{1,2,0:T(8,128)S(1)}, f32[4,4,168]{1,2,0:T(8,128)S(1)}, u32[]{:S(2)}, u32[]{:S(2)}) collective-permute-start(f32[4,4,168]{1,2,0:T(8,128)S(1)} %copy.55), channel_id=1, source_target_pairs={{1,120},{2,121},{3,122},{4,123},{5,124},{6,125},{7,126},{9,0},{10,... | collective-permute-start | bytes 32264 | tf_op jit(solution)/shard_map/ppermute | solution.py:37
  103.6 17.2 %collective-permute-start.7 = (f32[4,4,168]{1,2,0:T(8,128)S(1)}, f32[4,4,168]{1,2,0:T(8,128)S(1)}, u32[]{:S(2)}, u32[]{:S(2)}) collective-permute-start(f32[4,4,168]{1,2,0:T(8,128)S(1)} %copy.56), channel_id=1, source_target_pairs={{1,8},{2,9},{3,10},{4,11},{5,12},{6,13},{7,14},{9,16},{10,17},{11,... | collective-permute-start | bytes 32264 | tf_op jit(solution)/shard_map/ppermute | solution.py:37
where the time goes:
time: 222 us; the launch traced here: 221 us
  Pallas kernels  92.6 us (42%)
  waiting for transfers between devices  40.2 us (18%)
  starting transfers between devices  34.1 us (15%)
  other arithmetic  33.9 us (15%)
  local copies, waits for them, and re-layouts  20.1 us (9%)
    pallas_call x1, Pallas kernels, run_passes(): pl.pallas_call(passes_kernel, out_shape=jax.ShapeDtypeStruct((rows, chans...  92.6 us
    ppermute x4, waiting for transfers between devices, shift_both(): return lax.ppermute(block, ('lon', 'lat'), pairs)  21.2 us
    scatter-add x1, other arithmetic, local(): field = base.at[where].add(got)  19.4 us
    all_to_all x1, waiting for transfers between devices, local(): lax.all_to_all(send.reshape(devices, capacity, CPAD), ('lon', 'lat'), 0,...  19 us
    ppermute x4, starting transfers between devices, shift_both(): return lax.ppermute(block, ('lon', 'lat'), pairs)  17.5 us
    all_to_all x1, starting transfers between devices, local(): lax.all_to_all(send.reshape(devices, capacity, CPAD), ('lon', 'lat'), 0,...  10.2 us
    concatenate x1, other arithmetic, local(): jnp.concatenate([jnp.zeros((rows_y * cols_x, CPAD), jnp.float32), stat, j...  6.79 us
    ppermute x2, starting transfers between devices, shift_lat(): lax.ppermute(block, 'lat', [(i, i + step) for i in range(count) if 0 <= i...  5.84 us
  transfers between devices with their start and end apart: 9, of which 4 were waited for; matrix products, arithmetic and copies ran while one was open for 7% of the time, Pallas kernels for 0%

commit v1 on v0

--- a/solution.py
+++ b/solution.py
@@ -247,9 +247,11 @@
         axis=1,
     )
     send = jnp.zeros((devices * capacity, CPAD), jnp.float32).at[destination].set(payload)
-    got = lax.all_to_all(
-        send.reshape(devices, capacity, CPAD), ("lon", "lat"), 0, 0, tiled=True
-    ).reshape(devices * capacity, CPAD)
+    block = capacity * CPAD
+    shape = (devices, block // 128, 128) if block % 128 == 0 else (devices, capacity, CPAD)
+    got = lax.all_to_all(send.reshape(shape), ("lon", "lat"), 0, 0, tiled=True).reshape(
+        devices * capacity, CPAD
+    )
     where = got[:, CPAD - 1].astype(jnp.int32)
     got = jnp.pad(got, ((0, 0), (0, SPAD)))
     field = base.at[where].add(got)

time: 222 us -> 224 us (level)
  local copies, waits for them, and re-layouts: 20.1 us -> 26.6 us
  waiting for transfers between devices: 40.2 us -> 36.6 us
    reshape x0 -> x2, local copies, waits for them, and re-layouts: none -> 7.38 us  [the longest x1 3.91 us: local(): lax.all_to_all(send.reshape(shape), ('lon', 'lat'), 0, 0, tiled=True)]
    all_to_all x1, waiting for transfers between devices: 19 us -> 13.1 us  [local(): lax.all_to_all(send.reshape(shape), ('lon', 'lat'), 0, 0, tiled=True)]
    ppermute x4, waiting for transfers between devices: 21.2 us -> 23.5 us  [shift_both(): return lax.ppermute(block, ('lon', 'lat'), pairs)]
  transfers between devices with their start and end apart: 9 -> 9, of which waited for: 4 -> 5; matrix products, arithmetic and copies ran while one was open for 7% -> 7% of each run, Pallas kernels for 0% -> 0%
where the time goes in v1:
time: 224 us; the launch traced here: 223 us
  Pallas kernels  92.6 us (41%)
  waiting for transfers between devices  36.6 us (16%)
  starting transfers between devices  34.4 us (15%)
  other arithmetic  32.8 us (15%)
  local copies, waits for them, and re-layouts  26.6 us (12%)
    pallas_call x1, Pallas kernels, run_passes(): pl.pallas_call(passes_kernel, out_shape=jax.ShapeDtypeStruct((rows, chans...  92.6 us
    ppermute x4, waiting for transfers between devices, shift_both(): return lax.ppermute(block, ('lon', 'lat'), pairs)  23.5 us
    scatter-add x1, other arithmetic, local(): field = base.at[where].add(got)  18.4 us
    ppermute x4, starting transfers between devices, shift_both(): return lax.ppermute(block, ('lon', 'lat'), pairs)  16.8 us
    all_to_all x1, waiting for transfers between devices, local(): lax.all_to_all(send.reshape(shape), ('lon', 'lat'), 0, 0, tiled=True)  13.1 us
    all_to_all x1, starting transfers between devices, local(): lax.all_to_all(send.reshape(shape), ('lon', 'lat'), 0, 0, tiled=True)  10.6 us
    concatenate x1, other arithmetic, local(): jnp.concatenate([jnp.zeros((rows_y * cols_x, CPAD), jnp.float32), stat, j...  6.79 us
    ppermute x2, starting transfers between devices, shift_lat(): lax.ppermute(block, 'lat', [(i, i + step) for i in range(count) if 0 <= i...  5.84 us
  transfers between devices with their start and end apart: 9, of which 5 were waited for; matrix products, arithmetic and copies ran while one was open for 7% of the time, Pallas kernels for 0%

profile of v1, /device:TPU:34, one launch (start us, length us, event | category | flops | bytes accessed | tf_op | source)
XLA Modules:
  0.0 223.2 jit_solution(10221864192228493478)
XLA Ops:
  0.0 0.8 copy.29
  0.8 0.2 fusion.7
  1.1 0.9 fusion.6
  2.0 0.7 compare_select_fusion.1
  2.7 0.7 convert_element_type.31
  3.4 0.1 pad.21.clone
  3.5 1.1 select_bitcast_fusion
  4.5 0.1 pad_maximum_fusion.3
  4.6 0.2 copy.31
  4.8 0.0 copy-start.2
  4.9 2.8 %scatter_custom_fusion = f32[2048,152]{1,0:T(8,128)S(1)} fusion(s32[512]{0:T(512)S(1)} %bitcast.58, f32[512,152]{1,0:T(8,128)S(1)} %copy.31, f32[]{:T(128)} %constant.13.clone.1), kind=kCustom, calls=%fused_computation.8 | custom fusion | bytes 1245188 | tf_op jit(solution)/shard_map/scatter | solution.py:249
  7.6 3.5 %reshape.53 = f32[128,19,128]{2,1,0:T(8,128)} reshape(f32[2048,152]{1,0:T(8,128)S(1)} %scatter_custom_fusion) | data formatting | bytes 2490368 | tf_op jit(solution)/shard_map/reshape | solution.py:252
  11.1 10.6 %all-to-all-start = ((f32[128,19,128]{2,1,0:T(8,128)}), f32[128,19,128]{2,1,0:T(8,128)}, u32[]{:S(2)}, u32[]{:S(2)}) async-start(f32[128,19,128]{2,1,0:T(8,128)} %reshape.53), calls=%async_computation | async-start | bytes 3145728 | tf_op jit(solution)/shard_map/all_to_all | solution.py:252
  21.8 2.7 %copy.28 = f32[64,128,10]{2,1,0:T(8,128)} copy(f32[64,128,10]{1,0,2:T(8,128)S(1)} %maximum_bitcast_fusion) | data formatting | bytes 655360 | tf_op jit(solution)/shard_map/transpose | solution.py:224
  24.5 0.1 pad.25.clone
  24.6 6.8 %maximum_maximum_fusion = f32[8192,168]{1,0:T(8,128)} fusion(f32[8192,10]{1,0:T(8,128)} %bitcast.37, f32[168]{0:T(256)S(1)} %pad.25.clone, f32[168]{0:T(256)S(1)} %pad.23.clone), kind=kLoop, calls=%fused_computation.2 | loop fusion | flops 2752512 | bytes 5834048 | tf_op jit(solution)/shard_map/concatenate | solution.py:225
  31.4 13.1 %all-to-all-done = f32[128,19,128]{2,1,0:T(8,128)} async-done(((f32[128,19,128]{2,1,0:T(8,128)}), f32[128,19,128]{2,1,0:T(8,128)}, u32[]{:S(2)}, u32[]{:S(2)}) %all-to-all-start) | async-done | bytes 1245216 | tf_op jit(solution)/shard_map/all_to_all | solution.py:252
  44.5 3.9 %reshape.54 = f32[2048,152]{1,0:T(8,128)S(1)} reshape(f32[128,19,128]{2,1,0:T(8,128)} %all-to-all-done) | data formatting | bytes 2490368 | tf_op jit(solution)/shard_map/reshape | solution.py:252
  48.4 0.6 fusion.2
  49.0 18.4 %scatter_custom_fusion.1 = f32[8192,168]{1,0:T(8,128)} fusion(f32[8192,168]{1,0:T(8,128)} %maximum_maximum_fusion, s32[2048]{0:T(1024)S(1)} %fusion.2, f32[2048,152]{1,0:T(8,128)S(1)} %reshape.54, f32[]{:T(128)} %constant.13.clone.1), kind=kCustom, calls=%fused_computation.4 | custom fusion | flops 344064 | bytes 7602688 | tf_op jit(solution)/shard_map/scatter-add | solution.py:257
  67.4 1.3 fusion.11
  68.7 0.2 copy.36
  68.9 3.1 %collective-permute-start.2 = (f32[4,168,128]{2,1,0:T(8,128)S(1)}, f32[4,168,128]{2,1,0:T(8,128)S(1)}, u32[]{:S(2)}, u32[]{:S(2)}) collective-permute-start(f32[4,168,128]{2,1,0:T(8,128)S(1)} %bitcast.51), channel_id=1, source_target_pairs={{0,1},{1,2},{2,3},{3,4},{4,5},{5,6},{6,7},{8,9},{9,10},{10,11},{11... | collective-permute-start | bytes 1032200 | tf_op jit(solution)/shard_map/ppermute | solution.py:24
  72.1 0.2 copy.40
  72.3 2.7 %collective-permute-start.5 = (f32[4,168,128]{2,1,0:T(8,128)S(1)}, f32[4,168,128]{2,1,0:T(8,128)S(1)}, u32[]{:S(2)}, u32[]{:S(2)}) collective-permute-start(f32[4,168,128]{2,1,0:T(8,128)S(1)} %bitcast.52), channel_id=1, source_target_pairs={{1,0},{2,1},{3,2},{4,3},{5,4},{6,5},{7,6},{9,8},{10,9},{11,10},{12... | collective-permute-start | bytes 1032200 | tf_op jit(solution)/shard_map/ppermute | solution.py:24
  75.0 2.1 fusion.13
  77.1 1.2 collective-permute-start
  78.2 0.8 fusion.12
  79.1 0.2 copy.52
  79.2 6.8 %collective-permute-start.3 = (f32[4,4,168]{1,2,0:T(8,128)S(1)}, f32[4,4,168]{1,2,0:T(8,128)S(1)}, u32[]{:S(2)}, u32[]{:S(2)}) collective-permute-start(f32[4,4,168]{1,2,0:T(8,128)S(1)} %copy.52), channel_id=1, source_target_pairs={{0,121},{1,122},{2,123},{3,124},{4,125},{5,126},{6,127},{8,1},{9,2... | collective-permute-start | bytes 32264 | tf_op jit(solution)/shard_map/ppermute | solution.py:37
  86.1 0.1 pad.16.clone
  86.1 0.1 copy.43
  86.2 0.7 pad.9.bal_ref
  86.9 0.2 copy.53
  87.1 0.2 copy.54
  87.3 0.2 copy.55
  87.5 10.5 %collective-permute-done.3 = f32[4,4,168]{1,2,0:T(8,128)S(1)} collective-permute-done((f32[4,4,168]{1,2,0:T(8,128)S(1)}, f32[4,4,168]{1,2,0:T(8,128)S(1)}, u32[]{:S(2)}, u32[]{:S(2)}) %collective-permute-start.3) | collective-permute-done | bytes 10784 | tf_op jit(solution)/shard_map/ppermute | solution.py:37
  98.0 6.0 %collective-permute-start.4 = (f32[4,4,168]{1,2,0:T(8,128)S(1)}, f32[4,4,168]{1,2,0:T(8,128)S(1)}, u32[]{:S(2)}, u32[]{:S(2)}) collective-permute-start(f32[4,4,168]{1,2,0:T(8,128)S(1)} %copy.53), channel_id=1, source_target_pairs={{0,9},{1,10},{2,11},{3,12},{4,13},{5,14},{6,15},{8,17},{9,18},{10,... | collective-permute-start | bytes 32264 | tf_op jit(solution)/shard_map/ppermute | solution.py:37
  104.0 1.9 collective-permute-start.6
  105.9 2.1 collective-permute-start.7
  108.1 1.9 pad_maximum_fusion.2.ew_ref
  109.9 1.1 collective-permute-done.4
  111.1 3.9 %collective-permute-done.6 = f32[4,4,168]{1,2,0:T(8,128)S(1)} collective-permute-done((f32[4,4,168]{1,2,0:T(8,128)S(1)}, f32[4,4,168]{1,2,0:T(8,128)S(1)}, u32[]{:S(2)}, u32[]{:S(2)}) %collective-permute-start.6) | collective-permute-done | bytes 10784 | tf_op jit(solution)/shard_map/ppermute | solution.py:37
  115.0 7.9 %collective-permute-done.7 = f32[4,4,168]{1,2,0:T(8,128)S(1)} collective-permute-done((f32[4,4,168]{1,2,0:T(8,128)S(1)}, f32[4,4,168]{1,2,0:T(8,128)S(1)}, u32[]{:S(2)}, u32[]{:S(2)}) %collective-permute-start.7) | collective-permute-done | bytes 10784 | tf_op jit(solution)/shard_map/ppermute | solution.py:37
  122.9 1.4 pad_maximum_fusion.1
  124.2 0.8 broadcast_in_dim.40.lvl_ref
  125.0 92.6 %shard_map.73 = f32[64,150,128]{2,1,0:T(8,128)} custom-call(f32[64,128,168]{2,1,0:T(8,128)} %bitcast.40, f32[64,8,168]{2,1,0:T(8,128)} %pad_maximum_fusion.2.ew_ref, f32[4,168,256]{2,1,0:T(8,128)} %get-tuple-element.14.top_ref, f32[4,168,256]{2,1,0:T(8,128)} %get-tuple-element.13.bot_ref, f32[152,256]{1,0:T(8,128)} %broadcast_in_dim.40.lvl_ref, ...), custom_call_target="tpu_custom_call" | custom-call | flops 10444603392 | bytes 16121856 | tf_op jit(solution)/shard_map/pallas_call | solution.py:194
  217.6 5.6 %copy.45 = f32[150,64,128]{2,1,0:T(8,128)} copy(f32[150,64,128]{2,0,1:T(8,128)} %bitcast.41) | data formatting | bytes 9830400 | tf_op jit(solution)/shard_map/transpose | solution.py:260
  (24 shorter events, 0.2 us)
Async XLA Ops:
  4.8 16.9 %copy-start.2 = (s32[64,128]{1,0:T(8,128)S(1)}, s32[64,128]{1,0:T(8,128)}, u32[]{:S(2)}) copy-start(s32[64,128]{1,0:T(8,128)} %param.12) | copy-start | bytes 98308
  4.9 16.9 %copy-start = (f32[9,64,128]{2,1,0:T(8,128)S(1)}, f32[9,64,128]{2,1,0:T(8,128)}, u32[]{:S(2)}) copy-start(f32[9,64,128]{2,1,0:T(8,128)} %param.11) | copy-start | bytes 884740
  11.1 33.4 %all-to-all-start = ((f32[128,19,128]{2,1,0:T(8,128)}), f32[128,19,128]{2,1,0:T(8,128)}, u32[]{:S(2)}, u32[]{:S(2)}) async-start(f32[128,19,128]{2,1,0:T(8,128)} %reshape.53), calls=%async_computation | async-start | bytes 3145728 | tf_op jit(solution)/shard_map/all_to_all | solution.py:252
  67.4 18.7 %copy-start.1 = (f32[150,150]{1,0:T(8,128)S(1)}, f32[150,150]{1,0:T(8,128)}, u32[]{:S(2)}) copy-start(f32[150,150]{1,0:T(8,128)} %param.13) | copy-start | bytes 270004
  68.9 54.0 %collective-permute-start.2 = (f32[4,168,128]{2,1,0:T(8,128)S(1)}, f32[4,168,128]{2,1,0:T(8,128)S(1)}, u32[]{:S(2)}, u32[]{:S(2)}) collective-permute-start(f32[4,168,128]{2,1,0:T(8,128)S(1)} %bitcast.51), channel_id=1, source_target_pairs={{0,1},{1,2},{2,3},{3,4},{4,5},{5,6},{6,7},{8,9},{9,10},{10,11},{11... | collective-permute-start | bytes 1032200 | tf_op jit(solution)/shard_map/ppermute | solution.py:24
  72.3 50.6 %collective-permute-start.5 = (f32[4,168,128]{2,1,0:T(8,128)S(1)}, f32[4,168,128]{2,1,0:T(8,128)S(1)}, u32[]{:S(2)}, u32[]{:S(2)}) collective-permute-start(f32[4,168,128]{2,1,0:T(8,128)S(1)} %bitcast.52), channel_id=1, source_target_pairs={{1,0},{2,1},{3,2},{4,3},{5,4},{6,5},{7,6},{9,8},{10,9},{11,10},{12... | collective-permute-start | bytes 1032200 | tf_op jit(solution)/shard_map/ppermute | solution.py:24
  77.1 26.9 %collective-permute-start = (f32[64,4,168]{2,1,0:T(4,128)}, f32[64,4,168]{2,1,0:T(4,128)S(1)}, u32[]{:S(2)}, u32[]{:S(2)}) collective-permute-start(f32[64,4,168]{2,1,0:T(4,128)} %get-tuple-element.11), channel_id=1, source_target_pairs={{0,120},{8,0},{16,8},{24,16},{32,24},{40,32},{48,40},{56,48},{64,5... | collective-permute-start | bytes 516104 | tf_op jit(solution)/shard_map/ppermute | solution.py:19
  78.2 27.7 %collective-permute-start.1 = (f32[64,4,168]{2,1,0:T(4,128)}, f32[64,4,168]{2,1,0:T(4,128)}, u32[]{:S(2)}, u32[]{:S(2)}) collective-permute-start(f32[64,4,168]{2,1,0:T(4,128)} %get-tuple-element.12), channel_id=1, source_target_pairs={{0,8},{8,16},{16,24},{24,32},{32,40},{40,48},{48,56},{56,64},{64,7... | collective-permute-start | bytes 516104 | tf_op jit(solution)/shard_map/ppermute | solution.py:19
  79.2 18.7 %collective-permute-start.3 = (f32[4,4,168]{1,2,0:T(8,128)S(1)}, f32[4,4,168]{1,2,0:T(8,128)S(1)}, u32[]{:S(2)}, u32[]{:S(2)}) collective-permute-start(f32[4,4,168]{1,2,0:T(8,128)S(1)} %copy.52), channel_id=1, source_target_pairs={{0,121},{1,122},{2,123},{3,124},{4,125},{5,126},{6,127},{8,1},{9,2... | collective-permute-start | bytes 32264 | tf_op jit(solution)/shard_map/ppermute | solution.py:37
  98.0 13.1 %collective-permute-start.4 = (f32[4,4,168]{1,2,0:T(8,128)S(1)}, f32[4,4,168]{1,2,0:T(8,128)S(1)}, u32[]{:S(2)}, u32[]{:S(2)}) collective-permute-start(f32[4,4,168]{1,2,0:T(8,128)S(1)} %copy.53), channel_id=1, source_target_pairs={{0,9},{1,10},{2,11},{3,12},{4,13},{5,14},{6,15},{8,17},{9,18},{10,... | collective-permute-start | bytes 32264 | tf_op jit(solution)/shard_map/ppermute | solution.py:37
  104.0 11.0 %collective-permute-start.6 = (f32[4,4,168]{1,2,0:T(8,128)S(1)}, f32[4,4,168]{1,2,0:T(8,128)S(1)}, u32[]{:S(2)}, u32[]{:S(2)}) collective-permute-start(f32[4,4,168]{1,2,0:T(8,128)S(1)} %copy.54), channel_id=1, source_target_pairs={{1,120},{2,121},{3,122},{4,123},{5,124},{6,125},{7,126},{9,0},{10,... | collective-permute-start | bytes 32264 | tf_op jit(solution)/shard_map/ppermute | solution.py:37
  105.9 17.0 %collective-permute-start.7 = (f32[4,4,168]{1,2,0:T(8,128)S(1)}, f32[4,4,168]{1,2,0:T(8,128)S(1)}, u32[]{:S(2)}, u32[]{:S(2)}) collective-permute-start(f32[4,4,168]{1,2,0:T(8,128)S(1)} %copy.55), channel_id=1, source_target_pairs={{1,8},{2,9},{3,10},{4,11},{5,12},{6,13},{7,14},{9,16},{10,17},{11,... | collective-permute-start | bytes 32264 | tf_op jit(solution)/shard_map/ppermute | solution.py:37

commit v2 on v0

--- a/solution.py
+++ b/solution.py
@@ -132,7 +132,7 @@
             ref[y + RADIUS, :, LANES - RADIUS :] = sides[lo : lo + n, RADIUS:]
         return carry
 
-    lax.fori_loop(0, rows, fill, 0)
+    lax.fori_loop(0, rows, fill, 0, unroll=2)
     b_hi, b_lo = split_bf16(bal_ref[...])
     srcs = [p_ref, a_ref, b_ref, a_ref]
     dsts = [a_ref, b_ref, a_ref, None]
@@ -175,7 +175,7 @@
                 dst[y] = res
             return carry
 
-        lax.fori_loop(p + 1, full - 1 - p, row, 0, unroll=2)
+        lax.fori_loop(p + 1, full - 1 - p, row, 0, unroll=4)
 
 
 def run_passes(field, halos, balance, chans):

time: 222 us -> 208 us (0.937)
  Pallas kernels: 92.6 us -> 77.9 us
    pallas_call x1, Pallas kernels: 92.6 us -> 77.9 us  [run_passes(): pl.pallas_call(passes_kernel, out_shape=jax.ShapeDtypeStruct((rows, chans...]
  transfers between devices with their start and end apart: 9 -> 9, of which waited for: 4 -> 4; matrix products, arithmetic and copies ran while one was open for 7% -> 8% of each run, Pallas kernels for 0% -> 0%
where the time goes in v2:
time: 208 us; the launch traced here: 207 us
  Pallas kernels  77.9 us (37%)
  waiting for transfers between devices  39.7 us (19%)
  starting transfers between devices  35.2 us (17%)
  other arithmetic  33.5 us (16%)
  local copies, waits for them, and re-layouts  20.1 us (10%)
    pallas_call x1, Pallas kernels, run_passes(): pl.pallas_call(passes_kernel, out_shape=jax.ShapeDtypeStruct((rows, chans...  77.9 us
    ppermute x4, waiting for transfers between devices, shift_both(): return lax.ppermute(block, ('lon', 'lat'), pairs)  20.7 us
    scatter-add x1, other arithmetic, local(): field = base.at[where].add(got)  19.1 us
    all_to_all x1, waiting for transfers between devices, local(): lax.all_to_all(send.reshape(devices, capacity, CPAD), ('lon', 'lat'), 0,...  19 us
    ppermute x4, starting transfers between devices, shift_both(): return lax.ppermute(block, ('lon', 'lat'), pairs)  18.6 us
    all_to_all x1, starting transfers between devices, local(): lax.all_to_all(send.reshape(devices, capacity, CPAD), ('lon', 'lat'), 0,...  10.2 us
    concatenate x1, other arithmetic, local(): jnp.concatenate([jnp.zeros((rows_y * cols_x, CPAD), jnp.float32), stat, j...  6.79 us
    ppermute x2, starting transfers between devices, shift_lat(): lax.ppermute(block, 'lat', [(i, i + step) for i in range(count) if 0 <= i...  5.84 us
  transfers between devices with their start and end apart: 9, of which 4 were waited for; matrix products, arithmetic and copies ran while one was open for 8% of the time, Pallas kernels for 0%

profile of v2, /device:TPU:34, one launch (start us, length us, event | category | flops | bytes accessed | tf_op | source)
XLA Modules:
  0.0 206.7 jit_solution(9277294836297727499)
XLA Ops:
  0.0 0.8 copy.30
  0.8 0.2 fusion.7
  1.1 0.9 fusion.6
  2.0 0.7 compare_select_fusion.1
  2.7 0.7 convert_element_type.31
  3.4 0.1 pad.21.clone
  3.5 1.1 select_bitcast_fusion
  4.6 0.1 pad_maximum_fusion.3
  4.7 0.2 copy.32
  4.9 3.7 %scatter_custom_fusion = f32[2048,152]{1,0:T(8,128)} fusion(s32[512]{0:T(512)S(1)} %bitcast.63, f32[512,152]{1,0:T(8,128)S(1)} %copy.32, f32[]{:T(128)} %constant.13.clone.1), kind=kCustom, calls=%fused_computation.8 | custom fusion | bytes 1245188 | tf_op jit(solution)/shard_map/scatter | solution.py:249
  8.6 10.2 %all-to-all-start = ((f32[128,16,152]{2,1,0:T(8,128)}), f32[128,16,152]{2,1,0:T(8,128)S(1)}, u32[]{:S(2)}, u32[]{:S(2)}) async-start(f32[128,16,152]{2,1,0:T(8,128)} %bitcast.45), calls=%async_computation | async-start | bytes 4194304 | tf_op jit(solution)/shard_map/all_to_all | solution.py:250
  18.9 2.7 %copy.29 = f32[64,128,10]{2,1,0:T(8,128)} copy(f32[64,128,10]{1,0,2:T(8,128)S(1)} %maximum_bitcast_fusion) | data formatting | bytes 655360 | tf_op jit(solution)/shard_map/transpose | solution.py:224
  21.6 0.1 pad.25.clone
  21.7 6.8 %maximum_maximum_fusion = f32[8192,168]{1,0:T(8,128)} fusion(f32[8192,10]{1,0:T(8,128)} %bitcast.39, f32[168]{0:T(256)S(1)} %pad.25.clone, f32[168]{0:T(256)S(1)} %pad.23.clone), kind=kLoop, calls=%fused_computation.2 | loop fusion | flops 2752512 | bytes 5834048 | tf_op jit(solution)/shard_map/concatenate | solution.py:225
  28.5 19.0 %all-to-all-done = f32[128,16,152]{2,1,0:T(8,128)S(1)} async-done(((f32[128,16,152]{2,1,0:T(8,128)}), f32[128,16,152]{2,1,0:T(8,128)S(1)}, u32[]{:S(2)}, u32[]{:S(2)}) %all-to-all-start) | async-done | bytes 1245216 | tf_op jit(solution)/shard_map/all_to_all | solution.py:250
  47.5 0.6 fusion.2
  48.1 19.1 %scatter_custom_fusion.1 = f32[8192,168]{1,0:T(8,128)} fusion(f32[8192,168]{1,0:T(8,128)} %maximum_maximum_fusion, s32[2048]{0:T(1024)S(1)} %fusion.2, f32[2048,152]{1,0:T(8,128)S(1)} %bitcast.41, f32[]{:T(128)} %constant.13.clone.1), kind=kCustom, calls=%fused_computation.4 | custom fusion | flops 344064 | bytes 7602688 | tf_op jit(solution)/shard_map/scatter-add | solution.py:255
  67.2 1.3 fusion.11
  68.5 0.2 copy.37
  68.7 3.2 %collective-permute-start.2 = (f32[4,168,128]{2,1,0:T(8,128)S(1)}, f32[4,168,128]{2,1,0:T(8,128)S(1)}, u32[]{:S(2)}, u32[]{:S(2)}) collective-permute-start(f32[4,168,128]{2,1,0:T(8,128)S(1)} %bitcast.56), channel_id=1, source_target_pairs={{0,1},{1,2},{2,3},{3,4},{4,5},{5,6},{6,7},{8,9},{9,10},{10,11},{11... | collective-permute-start | bytes 1032200 | tf_op jit(solution)/shard_map/ppermute | solution.py:24
  71.9 0.2 copy.41
  72.1 2.6 %collective-permute-start.5 = (f32[4,168,128]{2,1,0:T(8,128)S(1)}, f32[4,168,128]{2,1,0:T(8,128)S(1)}, u32[]{:S(2)}, u32[]{:S(2)}) collective-permute-start(f32[4,168,128]{2,1,0:T(8,128)S(1)} %bitcast.57), channel_id=1, source_target_pairs={{1,0},{2,1},{3,2},{4,3},{5,4},{6,5},{7,6},{9,8},{10,9},{11,10},{12... | collective-permute-start | bytes 1032200 | tf_op jit(solution)/shard_map/ppermute | solution.py:24
  74.8 2.1 %fusion.13 = (f32[64,4,168]{2,1,0:T(4,128)}, f32[64,4,168]{2,1,0:T(4,128)}) fusion(f32[64,128,168]{2,1,0:T(8,128)} %bitcast.42), kind=kLoop, calls=%fused_computation.33 | loop fusion | bytes 688128 | tf_op jit(solution)/shard_map/slice | solution.py:81
  76.9 0.6 collective-permute-start
  77.5 0.0 collective-permute-start.1
  77.5 0.8 fusion.12
  78.3 0.2 copy.53
  78.5 7.0 %collective-permute-start.3 = (f32[4,4,168]{1,2,0:T(8,128)S(1)}, f32[4,4,168]{1,2,0:T(8,128)S(1)}, u32[]{:S(2)}, u32[]{:S(2)}) collective-permute-start(f32[4,4,168]{1,2,0:T(8,128)S(1)} %copy.53), channel_id=1, source_target_pairs={{0,121},{1,122},{2,123},{3,124},{4,125},{5,126},{6,127},{8,1},{9,2... | collective-permute-start | bytes 32264 | tf_op jit(solution)/shard_map/ppermute | solution.py:37
  85.5 0.1 pad.16.clone
  85.6 0.1 copy.44
  85.7 0.7 pad.9.bal_ref
  86.3 0.2 copy.54
  86.5 0.2 copy.55
  86.7 0.2 copy.56
  86.9 8.8 %collective-permute-done.3 = f32[4,4,168]{1,2,0:T(8,128)S(1)} collective-permute-done((f32[4,4,168]{1,2,0:T(8,128)S(1)}, f32[4,4,168]{1,2,0:T(8,128)S(1)}, u32[]{:S(2)}, u32[]{:S(2)}) %collective-permute-start.3) | collective-permute-done | bytes 10784 | tf_op jit(solution)/shard_map/ppermute | solution.py:37
  95.7 7.5 %collective-permute-start.4 = (f32[4,4,168]{1,2,0:T(8,128)S(1)}, f32[4,4,168]{1,2,0:T(8,128)S(1)}, u32[]{:S(2)}, u32[]{:S(2)}) collective-permute-start(f32[4,4,168]{1,2,0:T(8,128)S(1)} %copy.54), channel_id=1, source_target_pairs={{0,9},{1,10},{2,11},{3,12},{4,13},{5,14},{6,15},{8,17},{9,18},{10,... | collective-permute-start | bytes 32264 | tf_op jit(solution)/shard_map/ppermute | solution.py:37
  103.2 0.0 collective-permute-done
  103.3 1.9 collective-permute-start.6
  105.2 0.0 collective-permute-done.1
  105.2 2.1 %collective-permute-start.7 = (f32[4,4,168]{1,2,0:T(8,128)S(1)}, f32[4,4,168]{1,2,0:T(8,128)S(1)}, u32[]{:S(2)}, u32[]{:S(2)}) collective-permute-start(f32[4,4,168]{1,2,0:T(8,128)S(1)} %copy.56), channel_id=1, source_target_pairs={{1,8},{2,9},{3,10},{4,11},{5,12},{6,13},{7,14},{9,16},{10,17},{11,... | collective-permute-start | bytes 32264 | tf_op jit(solution)/shard_map/ppermute | solution.py:37
  107.3 1.9 pad_maximum_fusion.2.ew_ref
  109.2 0.0 collective-permute-done.4
  109.2 5.0 %collective-permute-done.6 = f32[4,4,168]{1,2,0:T(8,128)S(1)} collective-permute-done((f32[4,4,168]{1,2,0:T(8,128)S(1)}, f32[4,4,168]{1,2,0:T(8,128)S(1)}, u32[]{:S(2)}, u32[]{:S(2)}) %collective-permute-start.6) | collective-permute-done | bytes 10784 | tf_op jit(solution)/shard_map/ppermute | solution.py:37
  114.2 6.9 %collective-permute-done.7 = f32[4,4,168]{1,2,0:T(8,128)S(1)} collective-permute-done((f32[4,4,168]{1,2,0:T(8,128)S(1)}, f32[4,4,168]{1,2,0:T(8,128)S(1)}, u32[]{:S(2)}, u32[]{:S(2)}) %collective-permute-start.7) | collective-permute-done | bytes 10784 | tf_op jit(solution)/shard_map/ppermute | solution.py:37
  121.1 1.4 pad_maximum_fusion.1
  122.5 0.8 broadcast_in_dim.40.lvl_ref
  123.2 77.9 %shard_map.73 = f32[64,150,128]{2,1,0:T(8,128)} custom-call(f32[64,128,168]{2,1,0:T(8,128)} %bitcast.44, f32[64,8,168]{2,1,0:T(8,128)} %pad_maximum_fusion.2.ew_ref, f32[4,168,256]{2,1,0:T(8,128)} %get-tuple-element.14.top_ref, f32[4,168,256]{2,1,0:T(8,128)} %get-tuple-element.13.bot_ref, f32[152,256]{1,0:T(8,128)} %broadcast_in_dim.40.lvl_ref, ...), custom_call_target="tpu_custom_call" | custom-call | flops 10444603392 | bytes 16121856 | tf_op jit(solution)/shard_map/pallas_call | solution.py:194
  201.1 5.6 %copy.46 = f32[150,64,128]{2,1,0:T(8,128)} copy(f32[150,64,128]{2,0,1:T(8,128)} %bitcast.46) | data formatting | bytes 9830400 | tf_op jit(solution)/shard_map/transpose | solution.py:258
  (22 shorter events, 0.2 us)
Async XLA Ops:
  3.4 15.4 %copy-start.2 = (s32[64,128]{1,0:T(8,128)S(1)}, s32[64,128]{1,0:T(8,128)}, u32[]{:S(2)}) copy-start(s32[64,128]{1,0:T(8,128)} %param.12) | copy-start | bytes 98308
  3.5 15.4 %copy-start = (f32[9,64,128]{2,1,0:T(8,128)S(1)}, f32[9,64,128]{2,1,0:T(8,128)}, u32[]{:S(2)}) copy-start(f32[9,64,128]{2,1,0:T(8,128)} %param.11) | copy-start | bytes 884740
  8.6 38.9 %all-to-all-start = ((f32[128,16,152]{2,1,0:T(8,128)}), f32[128,16,152]{2,1,0:T(8,128)S(1)}, u32[]{:S(2)}, u32[]{:S(2)}) async-start(f32[128,16,152]{2,1,0:T(8,128)} %bitcast.45), calls=%async_computation | async-start | bytes 4194304 | tf_op jit(solution)/shard_map/all_to_all | solution.py:250
  67.2 18.4 %copy-start.1 = (f32[150,150]{1,0:T(8,128)S(1)}, f32[150,150]{1,0:T(8,128)}, u32[]{:S(2)}) copy-start(f32[150,150]{1,0:T(8,128)} %param.13) | copy-start | bytes 270004
  68.7 52.4 %collective-permute-start.2 = (f32[4,168,128]{2,1,0:T(8,128)S(1)}, f32[4,168,128]{2,1,0:T(8,128)S(1)}, u32[]{:S(2)}, u32[]{:S(2)}) collective-permute-start(f32[4,168,128]{2,1,0:T(8,128)S(1)} %bitcast.56), channel_id=1, source_target_pairs={{0,1},{1,2},{2,3},{3,4},{4,5},{5,6},{6,7},{8,9},{9,10},{10,11},{11... | collective-permute-start | bytes 1032200 | tf_op jit(solution)/shard_map/ppermute | solution.py:24
  72.1 49.0 %collective-permute-start.5 = (f32[4,168,128]{2,1,0:T(8,128)S(1)}, f32[4,168,128]{2,1,0:T(8,128)S(1)}, u32[]{:S(2)}, u32[]{:S(2)}) collective-permute-start(f32[4,168,128]{2,1,0:T(8,128)S(1)} %bitcast.57), channel_id=1, source_target_pairs={{1,0},{2,1},{3,2},{4,3},{5,4},{6,5},{7,6},{9,8},{10,9},{11,10},{12... | collective-permute-start | bytes 1032200 | tf_op jit(solution)/shard_map/ppermute | solution.py:24
  76.9 26.4 %collective-permute-start = (f32[64,4,168]{2,1,0:T(4,128)}, f32[64,4,168]{2,1,0:T(4,128)S(1)}, u32[]{:S(2)}, u32[]{:S(2)}) collective-permute-start(f32[64,4,168]{2,1,0:T(4,128)} %get-tuple-element.11), channel_id=1, source_target_pairs={{0,120},{8,0},{16,8},{24,16},{32,24},{40,32},{48,40},{56,48},{64,5... | collective-permute-start | bytes 516104 | tf_op jit(solution)/shard_map/ppermute | solution.py:19
  77.5 27.7 %collective-permute-start.1 = (f32[64,4,168]{2,1,0:T(4,128)}, f32[64,4,168]{2,1,0:T(4,128)}, u32[]{:S(2)}, u32[]{:S(2)}) collective-permute-start(f32[64,4,168]{2,1,0:T(4,128)} %get-tuple-element.12), channel_id=1, source_target_pairs={{0,8},{8,16},{16,24},{24,32},{32,40},{40,48},{48,56},{56,64},{64,7... | collective-permute-start | bytes 516104 | tf_op jit(solution)/shard_map/ppermute | solution.py:19
  78.5 17.2 %collective-permute-start.3 = (f32[4,4,168]{1,2,0:T(8,128)S(1)}, f32[4,4,168]{1,2,0:T(8,128)S(1)}, u32[]{:S(2)}, u32[]{:S(2)}) collective-permute-start(f32[4,4,168]{1,2,0:T(8,128)S(1)} %copy.53), channel_id=1, source_target_pairs={{0,121},{1,122},{2,123},{3,124},{4,125},{5,126},{6,127},{8,1},{9,2... | collective-permute-start | bytes 32264 | tf_op jit(solution)/shard_map/ppermute | solution.py:37
  95.7 13.5 %collective-permute-start.4 = (f32[4,4,168]{1,2,0:T(8,128)S(1)}, f32[4,4,168]{1,2,0:T(8,128)S(1)}, u32[]{:S(2)}, u32[]{:S(2)}) collective-permute-start(f32[4,4,168]{1,2,0:T(8,128)S(1)} %copy.54), channel_id=1, source_target_pairs={{0,9},{1,10},{2,11},{3,12},{4,13},{5,14},{6,15},{8,17},{9,18},{10,... | collective-permute-start | bytes 32264 | tf_op jit(solution)/shard_map/ppermute | solution.py:37
  103.3 10.9 %collective-permute-start.6 = (f32[4,4,168]{1,2,0:T(8,128)S(1)}, f32[4,4,168]{1,2,0:T(8,128)S(1)}, u32[]{:S(2)}, u32[]{:S(2)}) collective-permute-start(f32[4,4,168]{1,2,0:T(8,128)S(1)} %copy.55), channel_id=1, source_target_pairs={{1,120},{2,121},{3,122},{4,123},{5,124},{6,125},{7,126},{9,0},{10,... | collective-permute-start | bytes 32264 | tf_op jit(solution)/shard_map/ppermute | solution.py:37
  105.2 15.9 %collective-permute-start.7 = (f32[4,4,168]{1,2,0:T(8,128)S(1)}, f32[4,4,168]{1,2,0:T(8,128)S(1)}, u32[]{:S(2)}, u32[]{:S(2)}) collective-permute-start(f32[4,4,168]{1,2,0:T(8,128)S(1)} %copy.56), channel_id=1, source_target_pairs={{1,8},{2,9},{3,10},{4,11},{5,12},{6,13},{7,14},{9,16},{10,17},{11,... | collective-permute-start | bytes 32264 | tf_op jit(solution)/shard_map/ppermute | solution.py:37

commit v3 on v2

--- a/solution.py
+++ b/solution.py
@@ -132,7 +132,7 @@
             ref[y + RADIUS, :, LANES - RADIUS :] = sides[lo : lo + n, RADIUS:]
         return carry
 
-    lax.fori_loop(0, rows, fill, 0, unroll=2)
+    lax.fori_loop(0, rows, fill, 0, unroll=4)
     b_hi, b_lo = split_bf16(bal_ref[...])
     srcs = [p_ref, a_ref, b_ref, a_ref]
     dsts = [a_ref, b_ref, a_ref, None]
@@ -175,7 +175,7 @@
                 dst[y] = res
             return carry
 
-        lax.fori_loop(p + 1, full - 1 - p, row, 0, unroll=4)
+        lax.fori_loop(p + 1, full - 1 - p, row, 0, unroll=8)
 
 
 def run_passes(field, halos, balance, chans):

time: 208 us -> 199 us (0.957)
  Pallas kernels: 77.9 us -> 70.3 us
    pallas_call x1, Pallas kernels: 77.9 us -> 70.3 us  [run_passes(): pl.pallas_call(passes_kernel, out_shape=jax.ShapeDtypeStruct((rows, chans...]
  transfers between devices with their start and end apart: 9 -> 9, of which waited for: 4 -> 5; matrix products, arithmetic and copies ran while one was open for 8% -> 8% of each run, Pallas kernels for 0% -> 0%
where the time goes in v3:
time: 199 us; the launch traced here: 198 us
  Pallas kernels  70.3 us (35%)
  waiting for transfers between devices  40 us (20%)
  starting transfers between devices  33.8 us (17%)
  other arithmetic  33.4 us (17%)
  local copies, waits for them, and re-layouts  20.1 us (10%)
    pallas_call x1, Pallas kernels, run_passes(): pl.pallas_call(passes_kernel, out_shape=jax.ShapeDtypeStruct((rows, chans...  70.3 us
    ppermute x4, waiting for transfers between devices, shift_both(): return lax.ppermute(block, ('lon', 'lat'), pairs)  21 us
    scatter-add x1, other arithmetic, local(): field = base.at[where].add(got)  19 us
    all_to_all x1, waiting for transfers between devices, local(): lax.all_to_all(send.reshape(devices, capacity, CPAD), ('lon', 'lat'), 0,...  19 us
    ppermute x4, starting transfers between devices, shift_both(): return lax.ppermute(block, ('lon', 'lat'), pairs)  17.3 us
    all_to_all x1, starting transfers between devices, local(): lax.all_to_all(send.reshape(devices, capacity, CPAD), ('lon', 'lat'), 0,...  10.2 us
    concatenate x1, other arithmetic, local(): jnp.concatenate([jnp.zeros((rows_y * cols_x, CPAD), jnp.float32), stat, j...  6.79 us
    ppermute x2, starting transfers between devices, shift_lat(): lax.ppermute(block, 'lat', [(i, i + step) for i in range(count) if 0 <= i...  5.84 us
  transfers between devices with their start and end apart: 9, of which 5 were waited for; matrix products, arithmetic and copies ran while one was open for 8% of the time, Pallas kernels for 0%

profile of v3, /device:TPU:34, one launch (start us, length us, event | category | flops | bytes accessed | tf_op | source)
XLA Modules:
  0.0 198.0 jit_solution(564808120535370825)
XLA Ops:
  0.0 0.8 copy.30
  0.8 0.2 fusion.7
  1.1 0.9 fusion.6
  2.0 0.7 compare_select_fusion.1
  2.7 0.7 convert_element_type.31
  3.4 0.1 pad.21.clone
  3.5 1.1 select_bitcast_fusion
  4.6 0.1 pad_maximum_fusion.3
  4.7 0.2 copy.32
  4.9 3.7 %scatter_custom_fusion = f32[2048,152]{1,0:T(8,128)} fusion(s32[512]{0:T(512)S(1)} %bitcast.63, f32[512,152]{1,0:T(8,128)S(1)} %copy.32, f32[]{:T(128)} %constant.13.clone.1), kind=kCustom, calls=%fused_computation.8 | custom fusion | bytes 1245188 | tf_op jit(solution)/shard_map/scatter | solution.py:249
  8.6 10.2 %all-to-all-start = ((f32[128,16,152]{2,1,0:T(8,128)}), f32[128,16,152]{2,1,0:T(8,128)S(1)}, u32[]{:S(2)}, u32[]{:S(2)}) async-start(f32[128,16,152]{2,1,0:T(8,128)} %bitcast.45), calls=%async_computation | async-start | bytes 4194304 | tf_op jit(solution)/shard_map/all_to_all | solution.py:250
  18.9 2.7 %copy.29 = f32[64,128,10]{2,1,0:T(8,128)} copy(f32[64,128,10]{1,0,2:T(8,128)S(1)} %maximum_bitcast_fusion) | data formatting | bytes 655360 | tf_op jit(solution)/shard_map/transpose | solution.py:224
  21.6 0.1 pad.25.clone
  21.7 6.8 %maximum_maximum_fusion = f32[8192,168]{1,0:T(8,128)} fusion(f32[8192,10]{1,0:T(8,128)} %bitcast.39, f32[168]{0:T(256)S(1)} %pad.25.clone, f32[168]{0:T(256)S(1)} %pad.23.clone), kind=kLoop, calls=%fused_computation.2 | loop fusion | flops 2752512 | bytes 5834048 | tf_op jit(solution)/shard_map/concatenate | solution.py:225
  28.5 19.0 %all-to-all-done = f32[128,16,152]{2,1,0:T(8,128)S(1)} async-done(((f32[128,16,152]{2,1,0:T(8,128)}), f32[128,16,152]{2,1,0:T(8,128)S(1)}, u32[]{:S(2)}, u32[]{:S(2)}) %all-to-all-start) | async-done | bytes 1245216 | tf_op jit(solution)/shard_map/all_to_all | solution.py:250
  47.5 0.6 fusion.2
  48.1 19.0 %scatter_custom_fusion.1 = f32[8192,168]{1,0:T(8,128)} fusion(f32[8192,168]{1,0:T(8,128)} %maximum_maximum_fusion, s32[2048]{0:T(1024)S(1)} %fusion.2, f32[2048,152]{1,0:T(8,128)S(1)} %bitcast.41, f32[]{:T(128)} %constant.13.clone.1), kind=kCustom, calls=%fused_computation.4 | custom fusion | flops 344064 | bytes 7602688 | tf_op jit(solution)/shard_map/scatter-add | solution.py:255
  67.1 1.3 fusion.11
  68.5 0.2 copy.37
  68.7 1.9 collective-permute-start.2
  70.6 0.2 copy.41
  70.8 3.9 %collective-permute-start.5 = (f32[4,168,128]{2,1,0:T(8,128)S(1)}, f32[4,168,128]{2,1,0:T(8,128)S(1)}, u32[]{:S(2)}, u32[]{:S(2)}) collective-permute-start(f32[4,168,128]{2,1,0:T(8,128)S(1)} %bitcast.57), channel_id=1, source_target_pairs={{1,0},{2,1},{3,2},{4,3},{5,4},{6,5},{7,6},{9,8},{10,9},{11,10},{12... | collective-permute-start | bytes 1032200 | tf_op jit(solution)/shard_map/ppermute | solution.py:24
  74.7 2.1 %fusion.13 = (f32[64,4,168]{2,1,0:T(4,128)}, f32[64,4,168]{2,1,0:T(4,128)}) fusion(f32[64,128,168]{2,1,0:T(8,128)} %bitcast.42), kind=kLoop, calls=%fused_computation.33 | loop fusion | bytes 688128 | tf_op jit(solution)/shard_map/slice | solution.py:81
  76.8 0.2 collective-permute-start
  77.0 0.3 collective-permute-start.1
  77.3 0.8 fusion.12
  78.1 0.2 copy.53
  78.3 7.5 %collective-permute-start.3 = (f32[4,4,168]{1,2,0:T(8,128)S(1)}, f32[4,4,168]{1,2,0:T(8,128)S(1)}, u32[]{:S(2)}, u32[]{:S(2)}) collective-permute-start(f32[4,4,168]{1,2,0:T(8,128)S(1)} %copy.53), channel_id=1, source_target_pairs={{0,121},{1,122},{2,123},{3,124},{4,125},{5,126},{6,127},{8,1},{9,2... | collective-permute-start | bytes 32264 | tf_op jit(solution)/shard_map/ppermute | solution.py:37
  85.9 0.1 pad.16.clone
  85.9 0.1 copy.44
  86.0 0.7 pad.9.bal_ref
  86.7 0.2 copy.54
  86.9 0.2 copy.55
  87.1 0.2 copy.56
  87.3 8.2 %collective-permute-done.3 = f32[4,4,168]{1,2,0:T(8,128)S(1)} collective-permute-done((f32[4,4,168]{1,2,0:T(8,128)S(1)}, f32[4,4,168]{1,2,0:T(8,128)S(1)}, u32[]{:S(2)}, u32[]{:S(2)}) %collective-permute-start.3) | collective-permute-done | bytes 10784 | tf_op jit(solution)/shard_map/ppermute | solution.py:37
  95.5 3.6 %collective-permute-start.4 = (f32[4,4,168]{1,2,0:T(8,128)S(1)}, f32[4,4,168]{1,2,0:T(8,128)S(1)}, u32[]{:S(2)}, u32[]{:S(2)}) collective-permute-start(f32[4,4,168]{1,2,0:T(8,128)S(1)} %copy.54), channel_id=1, source_target_pairs={{0,9},{1,10},{2,11},{3,12},{4,13},{5,14},{6,15},{8,17},{9,18},{10,... | collective-permute-start | bytes 32264 | tf_op jit(solution)/shard_map/ppermute | solution.py:37
  99.1 0.0 collective-permute-done
  99.1 4.1 %collective-permute-start.6 = (f32[4,4,168]{1,2,0:T(8,128)S(1)}, f32[4,4,168]{1,2,0:T(8,128)S(1)}, u32[]{:S(2)}, u32[]{:S(2)}) collective-permute-start(f32[4,4,168]{1,2,0:T(8,128)S(1)} %copy.55), channel_id=1, source_target_pairs={{1,120},{2,121},{3,122},{4,123},{5,124},{6,125},{7,126},{9,0},{10,... | collective-permute-start | bytes 32264 | tf_op jit(solution)/shard_map/ppermute | solution.py:37
  103.2 0.0 collective-permute-done.1
  103.2 2.1 %collective-permute-start.7 = (f32[4,4,168]{1,2,0:T(8,128)S(1)}, f32[4,4,168]{1,2,0:T(8,128)S(1)}, u32[]{:S(2)}, u32[]{:S(2)}) collective-permute-start(f32[4,4,168]{1,2,0:T(8,128)S(1)} %copy.56), channel_id=1, source_target_pairs={{1,8},{2,9},{3,10},{4,11},{5,12},{6,13},{7,14},{9,16},{10,17},{11,... | collective-permute-start | bytes 32264 | tf_op jit(solution)/shard_map/ppermute | solution.py:37
  105.3 1.9 pad_maximum_fusion.2.ew_ref
  107.2 0.4 collective-permute-done.4
  107.6 4.7 %collective-permute-done.6 = f32[4,4,168]{1,2,0:T(8,128)S(1)} collective-permute-done((f32[4,4,168]{1,2,0:T(8,128)S(1)}, f32[4,4,168]{1,2,0:T(8,128)S(1)}, u32[]{:S(2)}, u32[]{:S(2)}) %collective-permute-start.6) | collective-permute-done | bytes 10784 | tf_op jit(solution)/shard_map/ppermute | solution.py:37
  112.3 7.7 %collective-permute-done.7 = f32[4,4,168]{1,2,0:T(8,128)S(1)} collective-permute-done((f32[4,4,168]{1,2,0:T(8,128)S(1)}, f32[4,4,168]{1,2,0:T(8,128)S(1)}, u32[]{:S(2)}, u32[]{:S(2)}) %collective-permute-start.7) | collective-permute-done | bytes 10784 | tf_op jit(solution)/shard_map/ppermute | solution.py:37
  120.0 1.4 pad_maximum_fusion.1
  121.3 0.8 broadcast_in_dim.40.lvl_ref
  122.1 70.3 %shard_map.73 = f32[64,150,128]{2,1,0:T(8,128)} custom-call(f32[64,128,168]{2,1,0:T(8,128)} %bitcast.44, f32[64,8,168]{2,1,0:T(8,128)} %pad_maximum_fusion.2.ew_ref, f32[4,168,256]{2,1,0:T(8,128)} %get-tuple-element.14.top_ref, f32[4,168,256]{2,1,0:T(8,128)} %get-tuple-element.13.bot_ref, f32[152,256]{1,0:T(8,128)} %broadcast_in_dim.40.lvl_ref, ...), custom_call_target="tpu_custom_call" | custom-call | flops 10444603392 | bytes 16121856 | tf_op jit(solution)/shard_map/pallas_call | solution.py:194
  192.4 5.6 %copy.46 = f32[150,64,128]{2,1,0:T(8,128)} copy(f32[150,64,128]{2,0,1:T(8,128)} %bitcast.46) | data formatting | bytes 9830400 | tf_op jit(solution)/shard_map/transpose | solution.py:258
  (22 shorter events, 0.2 us)
Async XLA Ops:
  3.4 15.4 %copy-start.2 = (s32[64,128]{1,0:T(8,128)S(1)}, s32[64,128]{1,0:T(8,128)}, u32[]{:S(2)}) copy-start(s32[64,128]{1,0:T(8,128)} %param.12) | copy-start | bytes 98308
  3.5 15.4 %copy-start = (f32[9,64,128]{2,1,0:T(8,128)S(1)}, f32[9,64,128]{2,1,0:T(8,128)}, u32[]{:S(2)}) copy-start(f32[9,64,128]{2,1,0:T(8,128)} %param.11) | copy-start | bytes 884740
  8.6 38.9 %all-to-all-start = ((f32[128,16,152]{2,1,0:T(8,128)}), f32[128,16,152]{2,1,0:T(8,128)S(1)}, u32[]{:S(2)}, u32[]{:S(2)}) async-start(f32[128,16,152]{2,1,0:T(8,128)} %bitcast.45), calls=%async_computation | async-start | bytes 4194304 | tf_op jit(solution)/shard_map/all_to_all | solution.py:250
  67.1 18.8 %copy-start.1 = (f32[150,150]{1,0:T(8,128)S(1)}, f32[150,150]{1,0:T(8,128)}, u32[]{:S(2)}) copy-start(f32[150,150]{1,0:T(8,128)} %param.13) | copy-start | bytes 270004
  68.7 51.3 %collective-permute-start.2 = (f32[4,168,128]{2,1,0:T(8,128)S(1)}, f32[4,168,128]{2,1,0:T(8,128)S(1)}, u32[]{:S(2)}, u32[]{:S(2)}) collective-permute-start(f32[4,168,128]{2,1,0:T(8,128)S(1)} %bitcast.56), channel_id=1, source_target_pairs={{0,1},{1,2},{2,3},{3,4},{4,5},{5,6},{6,7},{8,9},{9,10},{10,11},{11... | collective-permute-start | bytes 1032200 | tf_op jit(solution)/shard_map/ppermute | solution.py:24
  70.8 49.2 %collective-permute-start.5 = (f32[4,168,128]{2,1,0:T(8,128)S(1)}, f32[4,168,128]{2,1,0:T(8,128)S(1)}, u32[]{:S(2)}, u32[]{:S(2)}) collective-permute-start(f32[4,168,128]{2,1,0:T(8,128)S(1)} %bitcast.57), channel_id=1, source_target_pairs={{1,0},{2,1},{3,2},{4,3},{5,4},{6,5},{7,6},{9,8},{10,9},{11,10},{12... | collective-permute-start | bytes 1032200 | tf_op jit(solution)/shard_map/ppermute | solution.py:24
  76.8 22.3 %collective-permute-start = (f32[64,4,168]{2,1,0:T(4,128)}, f32[64,4,168]{2,1,0:T(4,128)S(1)}, u32[]{:S(2)}, u32[]{:S(2)}) collective-permute-start(f32[64,4,168]{2,1,0:T(4,128)} %get-tuple-element.11), channel_id=1, source_target_pairs={{0,120},{8,0},{16,8},{24,16},{32,24},{40,32},{48,40},{56,48},{64,5... | collective-permute-start | bytes 516104 | tf_op jit(solution)/shard_map/ppermute | solution.py:19
  77.0 26.2 %collective-permute-start.1 = (f32[64,4,168]{2,1,0:T(4,128)}, f32[64,4,168]{2,1,0:T(4,128)}, u32[]{:S(2)}, u32[]{:S(2)}) collective-permute-start(f32[64,4,168]{2,1,0:T(4,128)} %get-tuple-element.12), channel_id=1, source_target_pairs={{0,8},{8,16},{16,24},{24,32},{32,40},{40,48},{48,56},{56,64},{64,7... | collective-permute-start | bytes 516104 | tf_op jit(solution)/shard_map/ppermute | solution.py:19
  78.3 17.2 %collective-permute-start.3 = (f32[4,4,168]{1,2,0:T(8,128)S(1)}, f32[4,4,168]{1,2,0:T(8,128)S(1)}, u32[]{:S(2)}, u32[]{:S(2)}) collective-permute-start(f32[4,4,168]{1,2,0:T(8,128)S(1)} %copy.53), channel_id=1, source_target_pairs={{0,121},{1,122},{2,123},{3,124},{4,125},{5,126},{6,127},{8,1},{9,2... | collective-permute-start | bytes 32264 | tf_op jit(solution)/shard_map/ppermute | solution.py:37
  95.5 12.1 %collective-permute-start.4 = (f32[4,4,168]{1,2,0:T(8,128)S(1)}, f32[4,4,168]{1,2,0:T(8,128)S(1)}, u32[]{:S(2)}, u32[]{:S(2)}) collective-permute-start(f32[4,4,168]{1,2,0:T(8,128)S(1)} %copy.54), channel_id=1, source_target_pairs={{0,9},{1,10},{2,11},{3,12},{4,13},{5,14},{6,15},{8,17},{9,18},{10,... | collective-permute-start | bytes 32264 | tf_op jit(solution)/shard_map/ppermute | solution.py:37
  99.1 13.2 %collective-permute-start.6 = (f32[4,4,168]{1,2,0:T(8,128)S(1)}, f32[4,4,168]{1,2,0:T(8,128)S(1)}, u32[]{:S(2)}, u32[]{:S(2)}) collective-permute-start(f32[4,4,168]{1,2,0:T(8,128)S(1)} %copy.55), channel_id=1, source_target_pairs={{1,120},{2,121},{3,122},{4,123},{5,124},{6,125},{7,126},{9,0},{10,... | collective-permute-start | bytes 32264 | tf_op jit(solution)/shard_map/ppermute | solution.py:37
  103.2 16.8 %collective-permute-start.7 = (f32[4,4,168]{1,2,0:T(8,128)S(1)}, f32[4,4,168]{1,2,0:T(8,128)S(1)}, u32[]{:S(2)}, u32[]{:S(2)}) collective-permute-start(f32[4,4,168]{1,2,0:T(8,128)S(1)} %copy.56), channel_id=1, source_target_pairs={{1,8},{2,9},{3,10},{4,11},{5,12},{6,13},{7,14},{9,16},{10,17},{11,... | collective-permute-start | bytes 32264 | tf_op jit(solution)/shard_map/ppermute | solution.py:37

commit v4 on v3

--- a/solution.py
+++ b/solution.py
@@ -175,7 +175,7 @@
                 dst[y] = res
             return carry
 
-        lax.fori_loop(p + 1, full - 1 - p, row, 0, unroll=8)
+        lax.fori_loop(p + 1, full - 1 - p, row, 0, unroll=16)
 
 
 def run_passes(field, halos, balance, chans):

time: 199 us -> 196 us (0.985)
  Pallas kernels: 70.3 us -> 66.5 us
    pallas_call x1, Pallas kernels: 70.3 us -> 66.5 us  [run_passes(): pl.pallas_call(passes_kernel, out_shape=jax.ShapeDtypeStruct((rows, chans...]
where the time goes in v4:
time: 196 us; the launch traced here: 195 us
  Pallas kernels  66.5 us (34%)
  waiting for transfers between devices  41.2 us (21%)
  starting transfers between devices  34.7 us (18%)
  other arithmetic  32.6 us (17%)
  local copies, waits for them, and re-layouts  20.1 us (10%)
    pallas_call x1, Pallas kernels, run_passes(): pl.pallas_call(passes_kernel, out_shape=jax.ShapeDtypeStruct((rows, chans...  66.5 us
    ppermute x4, waiting for transfers between devices, shift_both(): return lax.ppermute(block, ('lon', 'lat'), pairs)  22.2 us
    all_to_all x1, waiting for transfers between devices, local(): lax.all_to_all(send.reshape(devices, capacity, CPAD), ('lon', 'lat'), 0,...  19 us
    scatter-add x1, other arithmetic, local(): field = base.at[where].add(got)  18.2 us
    ppermute x4, starting transfers between devices, shift_both(): return lax.ppermute(block, ('lon', 'lat'), pairs)  17.1 us
    all_to_all x1, starting transfers between devices, local(): lax.all_to_all(send.reshape(devices, capacity, CPAD), ('lon', 'lat'), 0,...  10.2 us
    concatenate x1, other arithmetic, local(): jnp.concatenate([jnp.zeros((rows_y * cols_x, CPAD), jnp.float32), stat, j...  6.79 us
    ppermute x2, starting transfers between devices, shift_lat(): lax.ppermute(block, 'lat', [(i, i + step) for i in range(count) if 0 <= i...  6.3 us
  transfers between devices with their start and end apart: 9, of which 5 were waited for; matrix products, arithmetic and copies ran while one was open for 8% of the time, Pallas kernels for 0%

profile of v4, /device:TPU:34, one launch (start us, length us, event | category | flops | bytes accessed | tf_op | source)
XLA Modules:
  0.0 195.4 jit_solution(1325629282963294867)
XLA Ops:
  0.0 0.8 copy.30
  0.8 0.2 fusion.7
  1.1 0.9 fusion.6
  2.0 0.7 compare_select_fusion.1
  2.7 0.7 convert_element_type.31
  3.4 0.1 pad.21.clone
  3.5 1.1 select_bitcast_fusion
  4.6 0.1 pad_maximum_fusion.3
  4.7 0.2 copy.32
  4.9 3.7 %scatter_custom_fusion = f32[2048,152]{1,0:T(8,128)} fusion(s32[512]{0:T(512)S(1)} %bitcast.63, f32[512,152]{1,0:T(8,128)S(1)} %copy.32, f32[]{:T(128)} %constant.13.clone.1), kind=kCustom, calls=%fused_computation.8 | custom fusion | bytes 1245188 | tf_op jit(solution)/shard_map/scatter | solution.py:249
  8.6 10.2 %all-to-all-start = ((f32[128,16,152]{2,1,0:T(8,128)}), f32[128,16,152]{2,1,0:T(8,128)S(1)}, u32[]{:S(2)}, u32[]{:S(2)}) async-start(f32[128,16,152]{2,1,0:T(8,128)} %bitcast.45), calls=%async_computation | async-start | bytes 4194304 | tf_op jit(solution)/shard_map/all_to_all | solution.py:250
  18.9 2.7 %copy.29 = f32[64,128,10]{2,1,0:T(8,128)} copy(f32[64,128,10]{1,0,2:T(8,128)S(1)} %maximum_bitcast_fusion) | data formatting | bytes 655360 | tf_op jit(solution)/shard_map/transpose | solution.py:224
  21.6 0.1 pad.25.clone
  21.7 6.8 %maximum_maximum_fusion = f32[8192,168]{1,0:T(8,128)} fusion(f32[8192,10]{1,0:T(8,128)} %bitcast.39, f32[168]{0:T(256)S(1)} %pad.25.clone, f32[168]{0:T(256)S(1)} %pad.23.clone), kind=kLoop, calls=%fused_computation.2 | loop fusion | flops 2752512 | bytes 5834048 | tf_op jit(solution)/shard_map/concatenate | solution.py:225
  28.5 19.0 %all-to-all-done = f32[128,16,152]{2,1,0:T(8,128)S(1)} async-done(((f32[128,16,152]{2,1,0:T(8,128)}), f32[128,16,152]{2,1,0:T(8,128)S(1)}, u32[]{:S(2)}, u32[]{:S(2)}) %all-to-all-start) | async-done | bytes 1245216 | tf_op jit(solution)/shard_map/all_to_all | solution.py:250
  47.5 0.6 fusion.2
  48.1 18.2 %scatter_custom_fusion.1 = f32[8192,168]{1,0:T(8,128)} fusion(f32[8192,168]{1,0:T(8,128)} %maximum_maximum_fusion, s32[2048]{0:T(1024)S(1)} %fusion.2, f32[2048,152]{1,0:T(8,128)S(1)} %bitcast.41, f32[]{:T(128)} %constant.13.clone.1), kind=kCustom, calls=%fused_computation.4 | custom fusion | flops 344064 | bytes 7602688 | tf_op jit(solution)/shard_map/scatter-add | solution.py:255
  66.3 1.3 fusion.11
  67.6 0.2 copy.37
  67.8 3.6 %collective-permute-start.2 = (f32[4,168,128]{2,1,0:T(8,128)S(1)}, f32[4,168,128]{2,1,0:T(8,128)S(1)}, u32[]{:S(2)}, u32[]{:S(2)}) collective-permute-start(f32[4,168,128]{2,1,0:T(8,128)S(1)} %bitcast.56), channel_id=1, source_target_pairs={{0,1},{1,2},{2,3},{3,4},{4,5},{5,6},{6,7},{8,9},{9,10},{10,11},{11... | collective-permute-start | bytes 1032200 | tf_op jit(solution)/shard_map/ppermute | solution.py:24
  71.4 0.2 copy.41
  71.6 2.7 %collective-permute-start.5 = (f32[4,168,128]{2,1,0:T(8,128)S(1)}, f32[4,168,128]{2,1,0:T(8,128)S(1)}, u32[]{:S(2)}, u32[]{:S(2)}) collective-permute-start(f32[4,168,128]{2,1,0:T(8,128)S(1)} %bitcast.57), channel_id=1, source_target_pairs={{1,0},{2,1},{3,2},{4,3},{5,4},{6,5},{7,6},{9,8},{10,9},{11,10},{12... | collective-permute-start | bytes 1032200 | tf_op jit(solution)/shard_map/ppermute | solution.py:24
  74.4 2.1 %fusion.13 = (f32[64,4,168]{2,1,0:T(4,128)}, f32[64,4,168]{2,1,0:T(4,128)}) fusion(f32[64,128,168]{2,1,0:T(8,128)} %bitcast.42), kind=kLoop, calls=%fused_computation.33 | loop fusion | bytes 688128 | tf_op jit(solution)/shard_map/slice | solution.py:81
  76.5 1.1 collective-permute-start
  77.5 0.0 collective-permute-start.1
  77.5 0.8 fusion.12
  78.4 0.2 copy.53
  78.5 7.0 %collective-permute-start.3 = (f32[4,4,168]{1,2,0:T(8,128)S(1)}, f32[4,4,168]{1,2,0:T(8,128)S(1)}, u32[]{:S(2)}, u32[]{:S(2)}) collective-permute-start(f32[4,4,168]{1,2,0:T(8,128)S(1)} %copy.53), channel_id=1, source_target_pairs={{0,121},{1,122},{2,123},{3,124},{4,125},{5,126},{6,127},{8,1},{9,2... | collective-permute-start | bytes 32264 | tf_op jit(solution)/shard_map/ppermute | solution.py:37
  85.6 0.1 pad.16.clone
  85.6 0.1 copy.44
  85.8 0.7 pad.9.bal_ref
  86.4 0.2 copy.54
  86.6 0.2 copy.55
  86.8 0.2 copy.56
  87.0 10.3 %collective-permute-done.3 = f32[4,4,168]{1,2,0:T(8,128)S(1)} collective-permute-done((f32[4,4,168]{1,2,0:T(8,128)S(1)}, f32[4,4,168]{1,2,0:T(8,128)S(1)}, u32[]{:S(2)}, u32[]{:S(2)}) %collective-permute-start.3) | collective-permute-done | bytes 10784 | tf_op jit(solution)/shard_map/ppermute | solution.py:37
  97.2 6.3 %collective-permute-start.4 = (f32[4,4,168]{1,2,0:T(8,128)S(1)}, f32[4,4,168]{1,2,0:T(8,128)S(1)}, u32[]{:S(2)}, u32[]{:S(2)}) collective-permute-start(f32[4,4,168]{1,2,0:T(8,128)S(1)} %copy.54), channel_id=1, source_target_pairs={{0,9},{1,10},{2,11},{3,12},{4,13},{5,14},{6,15},{8,17},{9,18},{10,... | collective-permute-start | bytes 32264 | tf_op jit(solution)/shard_map/ppermute | solution.py:37
  103.5 1.9 collective-permute-start.6
  105.5 0.0 collective-permute-done.1
  105.5 1.9 collective-permute-start.7
  107.4 1.9 pad_maximum_fusion.2.ew_ref
  109.3 1.3 collective-permute-done.4
  110.5 3.7 %collective-permute-done.6 = f32[4,4,168]{1,2,0:T(8,128)S(1)} collective-permute-done((f32[4,4,168]{1,2,0:T(8,128)S(1)}, f32[4,4,168]{1,2,0:T(8,128)S(1)}, u32[]{:S(2)}, u32[]{:S(2)}) %collective-permute-start.6) | collective-permute-done | bytes 10784 | tf_op jit(solution)/shard_map/ppermute | solution.py:37
  114.3 6.9 %collective-permute-done.7 = f32[4,4,168]{1,2,0:T(8,128)S(1)} collective-permute-done((f32[4,4,168]{1,2,0:T(8,128)S(1)}, f32[4,4,168]{1,2,0:T(8,128)S(1)}, u32[]{:S(2)}, u32[]{:S(2)}) %collective-permute-start.7) | collective-permute-done | bytes 10784 | tf_op jit(solution)/shard_map/ppermute | solution.py:37
  121.2 0.0 collective-permute-done.5
  121.2 1.4 pad_maximum_fusion.1
  122.6 0.8 broadcast_in_dim.40.lvl_ref
  123.3 66.5 %shard_map.73 = f32[64,150,128]{2,1,0:T(8,128)} custom-call(f32[64,128,168]{2,1,0:T(8,128)} %bitcast.44, f32[64,8,168]{2,1,0:T(8,128)} %pad_maximum_fusion.2.ew_ref, f32[4,168,256]{2,1,0:T(8,128)} %get-tuple-element.14.top_ref, f32[4,168,256]{2,1,0:T(8,128)} %get-tuple-element.13.bot_ref, f32[152,256]{1,0:T(8,128)} %broadcast_in_dim.40.lvl_ref, ...), custom_call_target="tpu_custom_call" | custom-call | flops 10444603392 | bytes 16121856 | tf_op jit(solution)/shard_map/pallas_call | solution.py:194
  189.8 5.6 %copy.46 = f32[150,64,128]{2,1,0:T(8,128)} copy(f32[150,64,128]{2,0,1:T(8,128)} %bitcast.46) | data formatting | bytes 9830400 | tf_op jit(solution)/shard_map/transpose | solution.py:258
  (22 shorter events, 0.2 us)
Async XLA Ops:
  3.4 15.4 %copy-start.2 = (s32[64,128]{1,0:T(8,128)S(1)}, s32[64,128]{1,0:T(8,128)}, u32[]{:S(2)}) copy-start(s32[64,128]{1,0:T(8,128)} %param.12) | copy-start | bytes 98308
  3.5 15.4 %copy-start = (f32[9,64,128]{2,1,0:T(8,128)S(1)}, f32[9,64,128]{2,1,0:T(8,128)}, u32[]{:S(2)}) copy-start(f32[9,64,128]{2,1,0:T(8,128)} %param.11) | copy-start | bytes 884740
  8.6 38.9 %all-to-all-start = ((f32[128,16,152]{2,1,0:T(8,128)}), f32[128,16,152]{2,1,0:T(8,128)S(1)}, u32[]{:S(2)}, u32[]{:S(2)}) async-start(f32[128,16,152]{2,1,0:T(8,128)} %bitcast.45), calls=%async_computation | async-start | bytes 4194304 | tf_op jit(solution)/shard_map/all_to_all | solution.py:250
  66.3 19.3 %copy-start.1 = (f32[150,150]{1,0:T(8,128)S(1)}, f32[150,150]{1,0:T(8,128)}, u32[]{:S(2)}) copy-start(f32[150,150]{1,0:T(8,128)} %param.13) | copy-start | bytes 270004
  67.8 53.4 %collective-permute-start.2 = (f32[4,168,128]{2,1,0:T(8,128)S(1)}, f32[4,168,128]{2,1,0:T(8,128)S(1)}, u32[]{:S(2)}, u32[]{:S(2)}) collective-permute-start(f32[4,168,128]{2,1,0:T(8,128)S(1)} %bitcast.56), channel_id=1, source_target_pairs={{0,1},{1,2},{2,3},{3,4},{4,5},{5,6},{6,7},{8,9},{9,10},{10,11},{11... | collective-permute-start | bytes 1032200 | tf_op jit(solution)/shard_map/ppermute | solution.py:24
  71.6 49.6 %collective-permute-start.5 = (f32[4,168,128]{2,1,0:T(8,128)S(1)}, f32[4,168,128]{2,1,0:T(8,128)S(1)}, u32[]{:S(2)}, u32[]{:S(2)}) collective-permute-start(f32[4,168,128]{2,1,0:T(8,128)S(1)} %bitcast.57), channel_id=1, source_target_pairs={{1,0},{2,1},{3,2},{4,3},{5,4},{6,5},{7,6},{9,8},{10,9},{11,10},{12... | collective-permute-start | bytes 1032200 | tf_op jit(solution)/shard_map/ppermute | solution.py:24
  76.5 27.1 %collective-permute-start = (f32[64,4,168]{2,1,0:T(4,128)}, f32[64,4,168]{2,1,0:T(4,128)S(1)}, u32[]{:S(2)}, u32[]{:S(2)}) collective-permute-start(f32[64,4,168]{2,1,0:T(4,128)} %get-tuple-element.11), channel_id=1, source_target_pairs={{0,120},{8,0},{16,8},{24,16},{32,24},{40,32},{48,40},{56,48},{64,5... | collective-permute-start | bytes 516104 | tf_op jit(solution)/shard_map/ppermute | solution.py:19
  77.5 27.9 %collective-permute-start.1 = (f32[64,4,168]{2,1,0:T(4,128)}, f32[64,4,168]{2,1,0:T(4,128)}, u32[]{:S(2)}, u32[]{:S(2)}) collective-permute-start(f32[64,4,168]{2,1,0:T(4,128)} %get-tuple-element.12), channel_id=1, source_target_pairs={{0,8},{8,16},{16,24},{24,32},{32,40},{40,48},{48,56},{56,64},{64,7... | collective-permute-start | bytes 516104 | tf_op jit(solution)/shard_map/ppermute | solution.py:19
  78.5 18.7 %collective-permute-start.3 = (f32[4,4,168]{1,2,0:T(8,128)S(1)}, f32[4,4,168]{1,2,0:T(8,128)S(1)}, u32[]{:S(2)}, u32[]{:S(2)}) collective-permute-start(f32[4,4,168]{1,2,0:T(8,128)S(1)} %copy.53), channel_id=1, source_target_pairs={{0,121},{1,122},{2,123},{3,124},{4,125},{5,126},{6,127},{8,1},{9,2... | collective-permute-start | bytes 32264 | tf_op jit(solution)/shard_map/ppermute | solution.py:37
  97.2 13.3 %collective-permute-start.4 = (f32[4,4,168]{1,2,0:T(8,128)S(1)}, f32[4,4,168]{1,2,0:T(8,128)S(1)}, u32[]{:S(2)}, u32[]{:S(2)}) collective-permute-start(f32[4,4,168]{1,2,0:T(8,128)S(1)} %copy.54), channel_id=1, source_target_pairs={{0,9},{1,10},{2,11},{3,12},{4,13},{5,14},{6,15},{8,17},{9,18},{10,... | collective-permute-start | bytes 32264 | tf_op jit(solution)/shard_map/ppermute | solution.py:37
  103.5 10.7 %collective-permute-start.6 = (f32[4,4,168]{1,2,0:T(8,128)S(1)}, f32[4,4,168]{1,2,0:T(8,128)S(1)}, u32[]{:S(2)}, u32[]{:S(2)}) collective-permute-start(f32[4,4,168]{1,2,0:T(8,128)S(1)} %copy.55), channel_id=1, source_target_pairs={{1,120},{2,121},{3,122},{4,123},{5,124},{6,125},{7,126},{9,0},{10,... | collective-permute-start | bytes 32264 | tf_op jit(solution)/shard_map/ppermute | solution.py:37
  105.5 15.7 %collective-permute-start.7 = (f32[4,4,168]{1,2,0:T(8,128)S(1)}, f32[4,4,168]{1,2,0:T(8,128)S(1)}, u32[]{:S(2)}, u32[]{:S(2)}) collective-permute-start(f32[4,4,168]{1,2,0:T(8,128)S(1)} %copy.56), channel_id=1, source_target_pairs={{1,8},{2,9},{3,10},{4,11},{5,12},{6,13},{7,14},{9,16},{10,17},{11,... | collective-permute-start | bytes 32264 | tf_op jit(solution)/shard_map/ppermute | solution.py:37

commit v5 on v4

--- a/solution.py
+++ b/solution.py
@@ -175,7 +175,9 @@
                 dst[y] = res
             return carry
 
-        lax.fori_loop(p + 1, full - 1 - p, row, 0, unroll=16)
+        count = full - 2 - 2 * p
+        unroll = max(d for d in range(1, 18) if count % d == 0)
+        lax.fori_loop(p + 1, full - 1 - p, row, 0, unroll=unroll)
 
 
 def run_passes(field, halos, balance, chans):

time: 196 us -> 194 us (0.990); the launches traced: 195 us -> 191 us
  starting transfers between devices: 34.7 us -> 32.7 us
  waiting for transfers between devices: 41.2 us -> 39.2 us
    ppermute x4, waiting for transfers between devices: 22.2 us -> 20.2 us  [shift_both(): return lax.ppermute(block, ('lon', 'lat'), pairs)]
where the time goes in v5:
time: 194 us; the launch traced here: 191 us
  Pallas kernels  65 us (34%)
  waiting for transfers between devices  39.2 us (20%)
  other arithmetic  34 us (18%)
  starting transfers between devices  32.7 us (17%)
  local copies, waits for them, and re-layouts  20.1 us (10%)
    pallas_call x1, Pallas kernels, run_passes(): pl.pallas_call(passes_kernel, out_shape=jax.ShapeDtypeStruct((rows, chans...  65 us
    ppermute x4, waiting for transfers between devices, shift_both(): return lax.ppermute(block, ('lon', 'lat'), pairs)  20.2 us
    scatter-add x1, other arithmetic, local(): field = base.at[where].add(got)  19.6 us
    all_to_all x1, waiting for transfers between devices, local(): lax.all_to_all(send.reshape(devices, capacity, CPAD), ('lon', 'lat'), 0,...  19 us
    ppermute x4, starting transfers between devices, shift_both(): return lax.ppermute(block, ('lon', 'lat'), pairs)  16.1 us
    all_to_all x1, starting transfers between devices, local(): lax.all_to_all(send.reshape(devices, capacity, CPAD), ('lon', 'lat'), 0,...  10.2 us
    concatenate x1, other arithmetic, local(): jnp.concatenate([jnp.zeros((rows_y * cols_x, CPAD), jnp.float32), stat, j...  6.79 us
    ppermute x2, starting transfers between devices, shift_lat(): lax.ppermute(block, 'lat', [(i, i + step) for i in range(count) if 0 <= i...  5.84 us
  transfers between devices with their start and end apart: 9, of which 5 were waited for; matrix products, arithmetic and copies ran while one was open for 8% of the time, Pallas kernels for 0%

profile of v5, /device:TPU:34, one launch (start us, length us, event | category | flops | bytes accessed | tf_op | source)
XLA Modules:
  0.0 191.2 jit_solution(9391637773548086272)
XLA Ops:
  0.0 0.8 copy.30
  0.8 0.2 fusion.7
  1.1 0.9 fusion.6
  2.0 0.7 compare_select_fusion.1
  2.7 0.7 convert_element_type.31
  3.4 0.1 pad.21.clone
  3.5 1.1 select_bitcast_fusion
  4.6 0.1 pad_maximum_fusion.3
  4.7 0.2 copy.32
  4.9 3.7 %scatter_custom_fusion = f32[2048,152]{1,0:T(8,128)} fusion(s32[512]{0:T(512)S(1)} %bitcast.63, f32[512,152]{1,0:T(8,128)S(1)} %copy.32, f32[]{:T(128)} %constant.13.clone.1), kind=kCustom, calls=%fused_computation.8 | custom fusion | bytes 1245188 | tf_op jit(solution)/shard_map/scatter | solution.py:251
  8.6 10.2 %all-to-all-start = ((f32[128,16,152]{2,1,0:T(8,128)}), f32[128,16,152]{2,1,0:T(8,128)S(1)}, u32[]{:S(2)}, u32[]{:S(2)}) async-start(f32[128,16,152]{2,1,0:T(8,128)} %bitcast.45), calls=%async_computation | async-start | bytes 4194304 | tf_op jit(solution)/shard_map/all_to_all | solution.py:252
  18.9 2.7 %copy.29 = f32[64,128,10]{2,1,0:T(8,128)} copy(f32[64,128,10]{1,0,2:T(8,128)S(1)} %maximum_bitcast_fusion) | data formatting | bytes 655360 | tf_op jit(solution)/shard_map/transpose | solution.py:226
  21.6 0.1 pad.25.clone
  21.7 6.8 %maximum_maximum_fusion = f32[8192,168]{1,0:T(8,128)} fusion(f32[8192,10]{1,0:T(8,128)} %bitcast.39, f32[168]{0:T(256)S(1)} %pad.25.clone, f32[168]{0:T(256)S(1)} %pad.23.clone), kind=kLoop, calls=%fused_computation.2 | loop fusion | flops 2752512 | bytes 5834048 | tf_op jit(solution)/shard_map/concatenate | solution.py:227
  28.5 19.0 %all-to-all-done = f32[128,16,152]{2,1,0:T(8,128)S(1)} async-done(((f32[128,16,152]{2,1,0:T(8,128)}), f32[128,16,152]{2,1,0:T(8,128)S(1)}, u32[]{:S(2)}, u32[]{:S(2)}) %all-to-all-start) | async-done | bytes 1245216 | tf_op jit(solution)/shard_map/all_to_all | solution.py:252
  47.5 0.6 fusion.2
  48.1 19.6 %scatter_custom_fusion.1 = f32[8192,168]{1,0:T(8,128)} fusion(f32[8192,168]{1,0:T(8,128)} %maximum_maximum_fusion, s32[2048]{0:T(1024)S(1)} %fusion.2, f32[2048,152]{1,0:T(8,128)S(1)} %bitcast.41, f32[]{:T(128)} %constant.13.clone.1), kind=kCustom, calls=%fused_computation.4 | custom fusion | flops 344064 | bytes 7602688 | tf_op jit(solution)/shard_map/scatter-add | solution.py:257
  67.7 1.3 fusion.11
  69.0 0.2 copy.37
  69.2 2.7 %collective-permute-start.2 = (f32[4,168,128]{2,1,0:T(8,128)S(1)}, f32[4,168,128]{2,1,0:T(8,128)S(1)}, u32[]{:S(2)}, u32[]{:S(2)}) collective-permute-start(f32[4,168,128]{2,1,0:T(8,128)S(1)} %bitcast.56), channel_id=1, source_target_pairs={{0,1},{1,2},{2,3},{3,4},{4,5},{5,6},{6,7},{8,9},{9,10},{10,11},{11... | collective-permute-start | bytes 1032200 | tf_op jit(solution)/shard_map/ppermute | solution.py:24
  71.9 0.2 copy.41
  72.1 3.2 %collective-permute-start.5 = (f32[4,168,128]{2,1,0:T(8,128)S(1)}, f32[4,168,128]{2,1,0:T(8,128)S(1)}, u32[]{:S(2)}, u32[]{:S(2)}) collective-permute-start(f32[4,168,128]{2,1,0:T(8,128)S(1)} %bitcast.57), channel_id=1, source_target_pairs={{1,0},{2,1},{3,2},{4,3},{5,4},{6,5},{7,6},{9,8},{10,9},{11,10},{12... | collective-permute-start | bytes 1032200 | tf_op jit(solution)/shard_map/ppermute | solution.py:24
  75.3 2.1 %fusion.13 = (f32[64,4,168]{2,1,0:T(4,128)}, f32[64,4,168]{2,1,0:T(4,128)}) fusion(f32[64,128,168]{2,1,0:T(8,128)} %bitcast.42), kind=kLoop, calls=%fused_computation.33 | loop fusion | bytes 688128 | tf_op jit(solution)/shard_map/slice | solution.py:81
  77.3 0.0 collective-permute-start
  77.3 0.5 collective-permute-start.1
  77.9 0.8 fusion.12
  78.7 0.2 copy.53
  78.9 6.4 %collective-permute-start.3 = (f32[4,4,168]{1,2,0:T(8,128)S(1)}, f32[4,4,168]{1,2,0:T(8,128)S(1)}, u32[]{:S(2)}, u32[]{:S(2)}) collective-permute-start(f32[4,4,168]{1,2,0:T(8,128)S(1)} %copy.53), channel_id=1, source_target_pairs={{0,121},{1,122},{2,123},{3,124},{4,125},{5,126},{6,127},{8,1},{9,2... | collective-permute-start | bytes 32264 | tf_op jit(solution)/shard_map/ppermute | solution.py:37
  85.3 0.1 pad.16.clone
  85.3 0.1 copy.44
  85.5 0.7 pad.9.bal_ref
  86.1 0.2 copy.54
  86.3 0.2 copy.55
  86.5 0.2 copy.56
  86.7 10.9 %collective-permute-done.3 = f32[4,4,168]{1,2,0:T(8,128)S(1)} collective-permute-done((f32[4,4,168]{1,2,0:T(8,128)S(1)}, f32[4,4,168]{1,2,0:T(8,128)S(1)}, u32[]{:S(2)}, u32[]{:S(2)}) %collective-permute-start.3) | collective-permute-done | bytes 10784 | tf_op jit(solution)/shard_map/ppermute | solution.py:37
  97.5 5.2 %collective-permute-start.4 = (f32[4,4,168]{1,2,0:T(8,128)S(1)}, f32[4,4,168]{1,2,0:T(8,128)S(1)}, u32[]{:S(2)}, u32[]{:S(2)}) collective-permute-start(f32[4,4,168]{1,2,0:T(8,128)S(1)} %copy.54), channel_id=1, source_target_pairs={{0,9},{1,10},{2,11},{3,12},{4,13},{5,14},{6,15},{8,17},{9,18},{10,... | collective-permute-start | bytes 32264 | tf_op jit(solution)/shard_map/ppermute | solution.py:37
  102.7 2.5 %collective-permute-start.6 = (f32[4,4,168]{1,2,0:T(8,128)S(1)}, f32[4,4,168]{1,2,0:T(8,128)S(1)}, u32[]{:S(2)}, u32[]{:S(2)}) collective-permute-start(f32[4,4,168]{1,2,0:T(8,128)S(1)} %copy.55), channel_id=1, source_target_pairs={{1,120},{2,121},{3,122},{4,123},{5,124},{6,125},{7,126},{9,0},{10,... | collective-permute-start | bytes 32264 | tf_op jit(solution)/shard_map/ppermute | solution.py:37
  105.2 0.0 collective-permute-done.1
  105.2 2.1 %collective-permute-start.7 = (f32[4,4,168]{1,2,0:T(8,128)S(1)}, f32[4,4,168]{1,2,0:T(8,128)S(1)}, u32[]{:S(2)}, u32[]{:S(2)}) collective-permute-start(f32[4,4,168]{1,2,0:T(8,128)S(1)} %copy.56), channel_id=1, source_target_pairs={{1,8},{2,9},{3,10},{4,11},{5,12},{6,13},{7,14},{9,16},{10,17},{11,... | collective-permute-start | bytes 32264 | tf_op jit(solution)/shard_map/ppermute | solution.py:37
  107.3 1.9 pad_maximum_fusion.2.ew_ref
  109.2 1.3 collective-permute-done.4
  110.5 3.6 %collective-permute-done.6 = f32[4,4,168]{1,2,0:T(8,128)S(1)} collective-permute-done((f32[4,4,168]{1,2,0:T(8,128)S(1)}, f32[4,4,168]{1,2,0:T(8,128)S(1)}, u32[]{:S(2)}, u32[]{:S(2)}) %collective-permute-start.6) | collective-permute-done | bytes 10784 | tf_op jit(solution)/shard_map/ppermute | solution.py:37
  114.1 4.4 %collective-permute-done.7 = f32[4,4,168]{1,2,0:T(8,128)S(1)} collective-permute-done((f32[4,4,168]{1,2,0:T(8,128)S(1)}, f32[4,4,168]{1,2,0:T(8,128)S(1)}, u32[]{:S(2)}, u32[]{:S(2)}) %collective-permute-start.7) | collective-permute-done | bytes 10784 | tf_op jit(solution)/shard_map/ppermute | solution.py:37
  118.5 0.0 collective-permute-done.2
  118.5 1.4 pad_maximum_fusion.1
  119.9 0.8 broadcast_in_dim.40.lvl_ref
  120.6 65.0 %shard_map.73 = f32[64,150,128]{2,1,0:T(8,128)} custom-call(f32[64,128,168]{2,1,0:T(8,128)} %bitcast.44, f32[64,8,168]{2,1,0:T(8,128)} %pad_maximum_fusion.2.ew_ref, f32[4,168,256]{2,1,0:T(8,128)} %get-tuple-element.14.top_ref, f32[4,168,256]{2,1,0:T(8,128)} %get-tuple-element.13.bot_ref, f32[152,256]{1,0:T(8,128)} %broadcast_in_dim.40.lvl_ref, ...), custom_call_target="tpu_custom_call" | custom-call | flops 10444603392 | bytes 16121856 | tf_op jit(solution)/shard_map/pallas_call | solution.py:196
  185.6 5.6 %copy.46 = f32[150,64,128]{2,1,0:T(8,128)} copy(f32[150,64,128]{2,0,1:T(8,128)} %bitcast.46) | data formatting | bytes 9830400 | tf_op jit(solution)/shard_map/transpose | solution.py:260
  (22 shorter events, 0.2 us)
Async XLA Ops:
  3.4 15.4 %copy-start.2 = (s32[64,128]{1,0:T(8,128)S(1)}, s32[64,128]{1,0:T(8,128)}, u32[]{:S(2)}) copy-start(s32[64,128]{1,0:T(8,128)} %param.12) | copy-start | bytes 98308
  3.5 15.4 %copy-start = (f32[9,64,128]{2,1,0:T(8,128)S(1)}, f32[9,64,128]{2,1,0:T(8,128)}, u32[]{:S(2)}) copy-start(f32[9,64,128]{2,1,0:T(8,128)} %param.11) | copy-start | bytes 884740
  8.6 38.9 %all-to-all-start = ((f32[128,16,152]{2,1,0:T(8,128)}), f32[128,16,152]{2,1,0:T(8,128)S(1)}, u32[]{:S(2)}, u32[]{:S(2)}) async-start(f32[128,16,152]{2,1,0:T(8,128)} %bitcast.45), calls=%async_computation | async-start | bytes 4194304 | tf_op jit(solution)/shard_map/all_to_all | solution.py:252
  67.7 17.7 %copy-start.1 = (f32[150,150]{1,0:T(8,128)S(1)}, f32[150,150]{1,0:T(8,128)}, u32[]{:S(2)}) copy-start(f32[150,150]{1,0:T(8,128)} %param.13) | copy-start | bytes 270004
  69.2 49.3 %collective-permute-start.2 = (f32[4,168,128]{2,1,0:T(8,128)S(1)}, f32[4,168,128]{2,1,0:T(8,128)S(1)}, u32[]{:S(2)}, u32[]{:S(2)}) collective-permute-start(f32[4,168,128]{2,1,0:T(8,128)S(1)} %bitcast.56), channel_id=1, source_target_pairs={{0,1},{1,2},{2,3},{3,4},{4,5},{5,6},{6,7},{8,9},{9,10},{10,11},{11... | collective-permute-start | bytes 1032200 | tf_op jit(solution)/shard_map/ppermute | solution.py:24
  72.1 46.4 %collective-permute-start.5 = (f32[4,168,128]{2,1,0:T(8,128)S(1)}, f32[4,168,128]{2,1,0:T(8,128)S(1)}, u32[]{:S(2)}, u32[]{:S(2)}) collective-permute-start(f32[4,168,128]{2,1,0:T(8,128)S(1)} %bitcast.57), channel_id=1, source_target_pairs={{1,0},{2,1},{3,2},{4,3},{5,4},{6,5},{7,6},{9,8},{10,9},{11,10},{12... | collective-permute-start | bytes 1032200 | tf_op jit(solution)/shard_map/ppermute | solution.py:24
  77.3 25.4 %collective-permute-start = (f32[64,4,168]{2,1,0:T(4,128)}, f32[64,4,168]{2,1,0:T(4,128)S(1)}, u32[]{:S(2)}, u32[]{:S(2)}) collective-permute-start(f32[64,4,168]{2,1,0:T(4,128)} %get-tuple-element.11), channel_id=1, source_target_pairs={{0,120},{8,0},{16,8},{24,16},{32,24},{40,32},{48,40},{56,48},{64,5... | collective-permute-start | bytes 516104 | tf_op jit(solution)/shard_map/ppermute | solution.py:19
  77.3 27.9 %collective-permute-start.1 = (f32[64,4,168]{2,1,0:T(4,128)}, f32[64,4,168]{2,1,0:T(4,128)}, u32[]{:S(2)}, u32[]{:S(2)}) collective-permute-start(f32[64,4,168]{2,1,0:T(4,128)} %get-tuple-element.12), channel_id=1, source_target_pairs={{0,8},{8,16},{16,24},{24,32},{32,40},{40,48},{48,56},{56,64},{64,7... | collective-permute-start | bytes 516104 | tf_op jit(solution)/shard_map/ppermute | solution.py:19
  78.9 18.7 %collective-permute-start.3 = (f32[4,4,168]{1,2,0:T(8,128)S(1)}, f32[4,4,168]{1,2,0:T(8,128)S(1)}, u32[]{:S(2)}, u32[]{:S(2)}) collective-permute-start(f32[4,4,168]{1,2,0:T(8,128)S(1)} %copy.53), channel_id=1, source_target_pairs={{0,121},{1,122},{2,123},{3,124},{4,125},{5,126},{6,127},{8,1},{9,2... | collective-permute-start | bytes 32264 | tf_op jit(solution)/shard_map/ppermute | solution.py:37
  97.5 13.0 %collective-permute-start.4 = (f32[4,4,168]{1,2,0:T(8,128)S(1)}, f32[4,4,168]{1,2,0:T(8,128)S(1)}, u32[]{:S(2)}, u32[]{:S(2)}) collective-permute-start(f32[4,4,168]{1,2,0:T(8,128)S(1)} %copy.54), channel_id=1, source_target_pairs={{0,9},{1,10},{2,11},{3,12},{4,13},{5,14},{6,15},{8,17},{9,18},{10,... | collective-permute-start | bytes 32264 | tf_op jit(solution)/shard_map/ppermute | solution.py:37
  102.7 11.4 %collective-permute-start.6 = (f32[4,4,168]{1,2,0:T(8,128)S(1)}, f32[4,4,168]{1,2,0:T(8,128)S(1)}, u32[]{:S(2)}, u32[]{:S(2)}) collective-permute-start(f32[4,4,168]{1,2,0:T(8,128)S(1)} %copy.55), channel_id=1, source_target_pairs={{1,120},{2,121},{3,122},{4,123},{5,124},{6,125},{7,126},{9,0},{10,... | collective-permute-start | bytes 32264 | tf_op jit(solution)/shard_map/ppermute | solution.py:37
  105.2 13.3 %collective-permute-start.7 = (f32[4,4,168]{1,2,0:T(8,128)S(1)}, f32[4,4,168]{1,2,0:T(8,128)S(1)}, u32[]{:S(2)}, u32[]{:S(2)}) collective-permute-start(f32[4,4,168]{1,2,0:T(8,128)S(1)} %copy.56), channel_id=1, source_target_pairs={{1,8},{2,9},{3,10},{4,11},{5,12},{6,13},{7,14},{9,16},{10,17},{11,... | collective-permute-start | bytes 32264 | tf_op jit(solution)/shard_map/ppermute | solution.py:37

commit v6 on v5

--- a/solution.py
+++ b/solution.py
@@ -132,7 +132,7 @@
             ref[y + RADIUS, :, LANES - RADIUS :] = sides[lo : lo + n, RADIUS:]
         return carry
 
-    lax.fori_loop(0, rows, fill, 0, unroll=4)
+    lax.fori_loop(0, rows, fill, 0, unroll=8)
     b_hi, b_lo = split_bf16(bal_ref[...])
     srcs = [p_ref, a_ref, b_ref, a_ref]
     dsts = [a_ref, b_ref, a_ref, None]

time: 194 us -> 194 us (level)
  no operation moved by 1% of the time
where the time goes in v6:
time: 194 us; the launch traced here: 191 us
  Pallas kernels  64 us (33%)
  waiting for transfers between devices  39.4 us (20%)
  other arithmetic  33.9 us (17%)
  starting transfers between devices  33.6 us (17%)
  local copies, waits for them, and re-layouts  20.1 us (10%)
    pallas_call x1, Pallas kernels, run_passes(): pl.pallas_call(passes_kernel, out_shape=jax.ShapeDtypeStruct((rows, chans...  64 us
    ppermute x4, waiting for transfers between devices, shift_both(): return lax.ppermute(block, ('lon', 'lat'), pairs)  20.4 us
    scatter-add x1, other arithmetic, local(): field = base.at[where].add(got)  19.5 us
    all_to_all x1, waiting for transfers between devices, local(): lax.all_to_all(send.reshape(devices, capacity, CPAD), ('lon', 'lat'), 0,...  19 us
    ppermute x4, starting transfers between devices, shift_both(): return lax.ppermute(block, ('lon', 'lat'), pairs)  17 us
    all_to_all x1, starting transfers between devices, local(): lax.all_to_all(send.reshape(devices, capacity, CPAD), ('lon', 'lat'), 0,...  10.2 us
    concatenate x1, other arithmetic, local(): jnp.concatenate([jnp.zeros((rows_y * cols_x, CPAD), jnp.float32), stat, j...  6.79 us
    ppermute x2, starting transfers between devices, shift_lat(): lax.ppermute(block, 'lat', [(i, i + step) for i in range(count) if 0 <= i...  5.84 us
  transfers between devices with their start and end apart: 9, of which 5 were waited for; matrix products, arithmetic and copies ran while one was open for 8% of the time, Pallas kernels for 0%

profile of v6, /device:TPU:34, one launch (start us, length us, event | category | flops | bytes accessed | tf_op | source)
XLA Modules:
  0.0 191.2 jit_solution(9494496105403619550)
XLA Ops:
  0.0 0.8 copy.30
  0.8 0.2 fusion.7
  1.1 0.9 fusion.6
  2.0 0.7 compare_select_fusion.1
  2.7 0.7 convert_element_type.31
  3.4 0.1 pad.21.clone
  3.5 1.1 select_bitcast_fusion
  4.6 0.1 pad_maximum_fusion.3
  4.7 0.2 copy.32
  4.9 3.7 %scatter_custom_fusion = f32[2048,152]{1,0:T(8,128)} fusion(s32[512]{0:T(512)S(1)} %bitcast.63, f32[512,152]{1,0:T(8,128)S(1)} %copy.32, f32[]{:T(128)} %constant.13.clone.1), kind=kCustom, calls=%fused_computation.8 | custom fusion | bytes 1245188 | tf_op jit(solution)/shard_map/scatter | solution.py:251
  8.6 10.2 %all-to-all-start = ((f32[128,16,152]{2,1,0:T(8,128)}), f32[128,16,152]{2,1,0:T(8,128)S(1)}, u32[]{:S(2)}, u32[]{:S(2)}) async-start(f32[128,16,152]{2,1,0:T(8,128)} %bitcast.45), calls=%async_computation | async-start | bytes 4194304 | tf_op jit(solution)/shard_map/all_to_all | solution.py:252
  18.9 2.7 %copy.29 = f32[64,128,10]{2,1,0:T(8,128)} copy(f32[64,128,10]{1,0,2:T(8,128)S(1)} %maximum_bitcast_fusion) | data formatting | bytes 655360 | tf_op jit(solution)/shard_map/transpose | solution.py:226
  21.6 0.1 pad.25.clone
  21.7 6.8 %maximum_maximum_fusion = f32[8192,168]{1,0:T(8,128)} fusion(f32[8192,10]{1,0:T(8,128)} %bitcast.39, f32[168]{0:T(256)S(1)} %pad.25.clone, f32[168]{0:T(256)S(1)} %pad.23.clone), kind=kLoop, calls=%fused_computation.2 | loop fusion | flops 2752512 | bytes 5834048 | tf_op jit(solution)/shard_map/concatenate | solution.py:227
  28.5 19.0 %all-to-all-done = f32[128,16,152]{2,1,0:T(8,128)S(1)} async-done(((f32[128,16,152]{2,1,0:T(8,128)}), f32[128,16,152]{2,1,0:T(8,128)S(1)}, u32[]{:S(2)}, u32[]{:S(2)}) %all-to-all-start) | async-done | bytes 1245216 | tf_op jit(solution)/shard_map/all_to_all | solution.py:252
  47.5 0.6 fusion.2
  48.1 19.5 %scatter_custom_fusion.1 = f32[8192,168]{1,0:T(8,128)} fusion(f32[8192,168]{1,0:T(8,128)} %maximum_maximum_fusion, s32[2048]{0:T(1024)S(1)} %fusion.2, f32[2048,152]{1,0:T(8,128)S(1)} %bitcast.41, f32[]{:T(128)} %constant.13.clone.1), kind=kCustom, calls=%fused_computation.4 | custom fusion | flops 344064 | bytes 7602688 | tf_op jit(solution)/shard_map/scatter-add | solution.py:257
  67.6 1.3 fusion.11
  68.9 0.2 copy.37
  69.1 1.9 %collective-permute-start.2 = (f32[4,168,128]{2,1,0:T(8,128)S(1)}, f32[4,168,128]{2,1,0:T(8,128)S(1)}, u32[]{:S(2)}, u32[]{:S(2)}) collective-permute-start(f32[4,168,128]{2,1,0:T(8,128)S(1)} %bitcast.56), channel_id=1, source_target_pairs={{0,1},{1,2},{2,3},{3,4},{4,5},{5,6},{6,7},{8,9},{9,10},{10,11},{11... | collective-permute-start | bytes 1032200 | tf_op jit(solution)/shard_map/ppermute | solution.py:24
  71.0 0.2 copy.41
  71.2 3.9 %collective-permute-start.5 = (f32[4,168,128]{2,1,0:T(8,128)S(1)}, f32[4,168,128]{2,1,0:T(8,128)S(1)}, u32[]{:S(2)}, u32[]{:S(2)}) collective-permute-start(f32[4,168,128]{2,1,0:T(8,128)S(1)} %bitcast.57), channel_id=1, source_target_pairs={{1,0},{2,1},{3,2},{4,3},{5,4},{6,5},{7,6},{9,8},{10,9},{11,10},{12... | collective-permute-start | bytes 1032200 | tf_op jit(solution)/shard_map/ppermute | solution.py:24
  75.2 2.1 %fusion.13 = (f32[64,4,168]{2,1,0:T(4,128)}, f32[64,4,168]{2,1,0:T(4,128)}) fusion(f32[64,128,168]{2,1,0:T(8,128)} %bitcast.42), kind=kLoop, calls=%fused_computation.33 | loop fusion | bytes 688128 | tf_op jit(solution)/shard_map/slice | solution.py:81
  77.2 0.1 collective-permute-start
  77.4 0.4 collective-permute-start.1
  77.8 0.8 fusion.12
  78.6 0.2 copy.53
  78.8 6.6 %collective-permute-start.3 = (f32[4,4,168]{1,2,0:T(8,128)S(1)}, f32[4,4,168]{1,2,0:T(8,128)S(1)}, u32[]{:S(2)}, u32[]{:S(2)}) collective-permute-start(f32[4,4,168]{1,2,0:T(8,128)S(1)} %copy.53), channel_id=1, source_target_pairs={{0,121},{1,122},{2,123},{3,124},{4,125},{5,126},{6,127},{8,1},{9,2... | collective-permute-start | bytes 32264 | tf_op jit(solution)/shard_map/ppermute | solution.py:37
  85.4 0.1 pad.16.clone
  85.5 0.1 copy.44
  85.6 0.7 pad.9.bal_ref
  86.3 0.2 copy.54
  86.5 0.2 copy.55
  86.6 0.2 copy.56
  86.8 9.1 %collective-permute-done.3 = f32[4,4,168]{1,2,0:T(8,128)S(1)} collective-permute-done((f32[4,4,168]{1,2,0:T(8,128)S(1)}, f32[4,4,168]{1,2,0:T(8,128)S(1)}, u32[]{:S(2)}, u32[]{:S(2)}) %collective-permute-start.3) | collective-permute-done | bytes 10784 | tf_op jit(solution)/shard_map/ppermute | solution.py:37
  95.9 6.4 %collective-permute-start.4 = (f32[4,4,168]{1,2,0:T(8,128)S(1)}, f32[4,4,168]{1,2,0:T(8,128)S(1)}, u32[]{:S(2)}, u32[]{:S(2)}) collective-permute-start(f32[4,4,168]{1,2,0:T(8,128)S(1)} %copy.54), channel_id=1, source_target_pairs={{0,9},{1,10},{2,11},{3,12},{4,13},{5,14},{6,15},{8,17},{9,18},{10,... | collective-permute-start | bytes 32264 | tf_op jit(solution)/shard_map/ppermute | solution.py:37
  102.3 0.0 collective-permute-done
  102.3 1.9 %collective-permute-start.6 = (f32[4,4,168]{1,2,0:T(8,128)S(1)}, f32[4,4,168]{1,2,0:T(8,128)S(1)}, u32[]{:S(2)}, u32[]{:S(2)}) collective-permute-start(f32[4,4,168]{1,2,0:T(8,128)S(1)} %copy.55), channel_id=1, source_target_pairs={{1,120},{2,121},{3,122},{4,123},{5,124},{6,125},{7,126},{9,0},{10,... | collective-permute-start | bytes 32264 | tf_op jit(solution)/shard_map/ppermute | solution.py:37
  104.2 0.0 collective-permute-done.1
  104.2 2.1 %collective-permute-start.7 = (f32[4,4,168]{1,2,0:T(8,128)S(1)}, f32[4,4,168]{1,2,0:T(8,128)S(1)}, u32[]{:S(2)}, u32[]{:S(2)}) collective-permute-start(f32[4,4,168]{1,2,0:T(8,128)S(1)} %copy.56), channel_id=1, source_target_pairs={{1,8},{2,9},{3,10},{4,11},{5,12},{6,13},{7,14},{9,16},{10,17},{11,... | collective-permute-start | bytes 32264 | tf_op jit(solution)/shard_map/ppermute | solution.py:37
  106.4 1.9 pad_maximum_fusion.2.ew_ref
  108.2 0.3 collective-permute-done.4
  108.6 5.6 %collective-permute-done.6 = f32[4,4,168]{1,2,0:T(8,128)S(1)} collective-permute-done((f32[4,4,168]{1,2,0:T(8,128)S(1)}, f32[4,4,168]{1,2,0:T(8,128)S(1)}, u32[]{:S(2)}, u32[]{:S(2)}) %collective-permute-start.6) | collective-permute-done | bytes 10784 | tf_op jit(solution)/shard_map/ppermute | solution.py:37
  114.1 5.4 %collective-permute-done.7 = f32[4,4,168]{1,2,0:T(8,128)S(1)} collective-permute-done((f32[4,4,168]{1,2,0:T(8,128)S(1)}, f32[4,4,168]{1,2,0:T(8,128)S(1)}, u32[]{:S(2)}, u32[]{:S(2)}) %collective-permute-start.7) | collective-permute-done | bytes 10784 | tf_op jit(solution)/shard_map/ppermute | solution.py:37
  119.5 1.4 pad_maximum_fusion.1
  120.9 0.8 broadcast_in_dim.40.lvl_ref
  121.6 64.0 %shard_map.73 = f32[64,150,128]{2,1,0:T(8,128)} custom-call(f32[64,128,168]{2,1,0:T(8,128)} %bitcast.44, f32[64,8,168]{2,1,0:T(8,128)} %pad_maximum_fusion.2.ew_ref, f32[4,168,256]{2,1,0:T(8,128)} %get-tuple-element.14.top_ref, f32[4,168,256]{2,1,0:T(8,128)} %get-tuple-element.13.bot_ref, f32[152,256]{1,0:T(8,128)} %broadcast_in_dim.40.lvl_ref, ...), custom_call_target="tpu_custom_call" | custom-call | flops 10444603392 | bytes 16121856 | tf_op jit(solution)/shard_map/pallas_call | solution.py:196
  185.6 5.6 %copy.46 = f32[150,64,128]{2,1,0:T(8,128)} copy(f32[150,64,128]{2,0,1:T(8,128)} %bitcast.46) | data formatting | bytes 9830400 | tf_op jit(solution)/shard_map/transpose | solution.py:260
  (22 shorter events, 0.2 us)
Async XLA Ops:
  3.4 15.4 %copy-start.2 = (s32[64,128]{1,0:T(8,128)S(1)}, s32[64,128]{1,0:T(8,128)}, u32[]{:S(2)}) copy-start(s32[64,128]{1,0:T(8,128)} %param.12) | copy-start | bytes 98308
  3.5 15.4 %copy-start = (f32[9,64,128]{2,1,0:T(8,128)S(1)}, f32[9,64,128]{2,1,0:T(8,128)}, u32[]{:S(2)}) copy-start(f32[9,64,128]{2,1,0:T(8,128)} %param.11) | copy-start | bytes 884740
  8.6 38.9 %all-to-all-start = ((f32[128,16,152]{2,1,0:T(8,128)}), f32[128,16,152]{2,1,0:T(8,128)S(1)}, u32[]{:S(2)}, u32[]{:S(2)}) async-start(f32[128,16,152]{2,1,0:T(8,128)} %bitcast.45), calls=%async_computation | async-start | bytes 4194304 | tf_op jit(solution)/shard_map/all_to_all | solution.py:252
  67.6 17.9 %copy-start.1 = (f32[150,150]{1,0:T(8,128)S(1)}, f32[150,150]{1,0:T(8,128)}, u32[]{:S(2)}) copy-start(f32[150,150]{1,0:T(8,128)} %param.13) | copy-start | bytes 270004
  69.1 50.4 %collective-permute-start.2 = (f32[4,168,128]{2,1,0:T(8,128)S(1)}, f32[4,168,128]{2,1,0:T(8,128)S(1)}, u32[]{:S(2)}, u32[]{:S(2)}) collective-permute-start(f32[4,168,128]{2,1,0:T(8,128)S(1)} %bitcast.56), channel_id=1, source_target_pairs={{0,1},{1,2},{2,3},{3,4},{4,5},{5,6},{6,7},{8,9},{9,10},{10,11},{11... | collective-permute-start | bytes 1032200 | tf_op jit(solution)/shard_map/ppermute | solution.py:24
  71.2 48.3 %collective-permute-start.5 = (f32[4,168,128]{2,1,0:T(8,128)S(1)}, f32[4,168,128]{2,1,0:T(8,128)S(1)}, u32[]{:S(2)}, u32[]{:S(2)}) collective-permute-start(f32[4,168,128]{2,1,0:T(8,128)S(1)} %bitcast.57), channel_id=1, source_target_pairs={{1,0},{2,1},{3,2},{4,3},{5,4},{6,5},{7,6},{9,8},{10,9},{11,10},{12... | collective-permute-start | bytes 1032200 | tf_op jit(solution)/shard_map/ppermute | solution.py:24
  77.2 25.1 %collective-permute-start = (f32[64,4,168]{2,1,0:T(4,128)}, f32[64,4,168]{2,1,0:T(4,128)S(1)}, u32[]{:S(2)}, u32[]{:S(2)}) collective-permute-start(f32[64,4,168]{2,1,0:T(4,128)} %get-tuple-element.11), channel_id=1, source_target_pairs={{0,120},{8,0},{16,8},{24,16},{32,24},{40,32},{48,40},{56,48},{64,5... | collective-permute-start | bytes 516104 | tf_op jit(solution)/shard_map/ppermute | solution.py:19
  77.4 26.8 %collective-permute-start.1 = (f32[64,4,168]{2,1,0:T(4,128)}, f32[64,4,168]{2,1,0:T(4,128)}, u32[]{:S(2)}, u32[]{:S(2)}) collective-permute-start(f32[64,4,168]{2,1,0:T(4,128)} %get-tuple-element.12), channel_id=1, source_target_pairs={{0,8},{8,16},{16,24},{24,32},{32,40},{40,48},{48,56},{56,64},{64,7... | collective-permute-start | bytes 516104 | tf_op jit(solution)/shard_map/ppermute | solution.py:19
  78.8 17.1 %collective-permute-start.3 = (f32[4,4,168]{1,2,0:T(8,128)S(1)}, f32[4,4,168]{1,2,0:T(8,128)S(1)}, u32[]{:S(2)}, u32[]{:S(2)}) collective-permute-start(f32[4,4,168]{1,2,0:T(8,128)S(1)} %copy.53), channel_id=1, source_target_pairs={{0,121},{1,122},{2,123},{3,124},{4,125},{5,126},{6,127},{8,1},{9,2... | collective-permute-start | bytes 32264 | tf_op jit(solution)/shard_map/ppermute | solution.py:37
  95.9 12.7 %collective-permute-start.4 = (f32[4,4,168]{1,2,0:T(8,128)S(1)}, f32[4,4,168]{1,2,0:T(8,128)S(1)}, u32[]{:S(2)}, u32[]{:S(2)}) collective-permute-start(f32[4,4,168]{1,2,0:T(8,128)S(1)} %copy.54), channel_id=1, source_target_pairs={{0,9},{1,10},{2,11},{3,12},{4,13},{5,14},{6,15},{8,17},{9,18},{10,... | collective-permute-start | bytes 32264 | tf_op jit(solution)/shard_map/ppermute | solution.py:37
  102.3 11.8 %collective-permute-start.6 = (f32[4,4,168]{1,2,0:T(8,128)S(1)}, f32[4,4,168]{1,2,0:T(8,128)S(1)}, u32[]{:S(2)}, u32[]{:S(2)}) collective-permute-start(f32[4,4,168]{1,2,0:T(8,128)S(1)} %copy.55), channel_id=1, source_target_pairs={{1,120},{2,121},{3,122},{4,123},{5,124},{6,125},{7,126},{9,0},{10,... | collective-permute-start | bytes 32264 | tf_op jit(solution)/shard_map/ppermute | solution.py:37
  104.2 15.3 %collective-permute-start.7 = (f32[4,4,168]{1,2,0:T(8,128)S(1)}, f32[4,4,168]{1,2,0:T(8,128)S(1)}, u32[]{:S(2)}, u32[]{:S(2)}) collective-permute-start(f32[4,4,168]{1,2,0:T(8,128)S(1)} %copy.56), channel_id=1, source_target_pairs={{1,8},{2,9},{3,10},{4,11},{5,12},{6,13},{7,14},{9,16},{10,17},{11,... | collective-permute-start | bytes 32264 | tf_op jit(solution)/shard_map/ppermute | solution.py:37
